TPU v7x, 128 devices: a whole 4x4x4 slice. The times are simulated.
128 devices in a mesh: dp: 8 (over x, core), table: 16 (over z, y).
Axes of the slice: x: 4, y: 4, z: 4, core: 2. Of those that a mesh axis runs over, the one named last changes fastest.
Arguments:
- user_table: bfloat16 [524288, 256], P(('dp', 'table')), may hold values from -6 to 6
- item_table: bfloat16 [524288, 256], P(('dp', 'table')), may hold values from -6 to 6
- hist_owner: int32 [262144, 1], P(('dp', 'table')), may hold values from 0 to 127; in each aligned block of 2048 rows (0 to 2047, 2048 to 4095, ...) at most 32 rows name the same one
- hist_row: int32 [262144], P(('dp', 'table')), may hold values from 0 to 4095
- hist_seg: int32 [128, 2048], P(('dp', 'table')), may hold values from 0 to 127, never falling along the last dimension, each value on 1 to 64 neighbouring positions
- hist_wix: int32 [262144], P(('dp', 'table')), may hold values from 0 to 63
- bag_weights: bfloat16 [64], replicated, may hold values from 0.099609375 to 1
- item_owner: int32 [16384, 1], P(('dp', 'table')), may hold values from 0 to 127; in each aligned block of 128 rows (0 to 127, 128 to 255, ...) at most 2 rows name the same one
- item_row: int32 [16384], P(('dp', 'table')), may hold values from 0 to 4095
- user_proj: bfloat16 [256, 256], replicated, may hold values from -0.375 to 0.375
- item_proj: bfloat16 [256, 256], replicated, may hold values from -0.375 to 0.375
- logit_scale: float32 [1], replicated, may hold values from 8 to 600
Outputs:
- user_grad: float32 [524288, 256], P(('dp', 'table'))
- item_grad: float32 [524288, 256], P(('dp', 'table'))
- user_proj_grad: float32 [256, 256], replicated
- item_proj_grad: float32 [256, 256], replicated
Inputs may be any that keep to these rules, and one draw needn't show every extreme that they name: `hist_owner`: among the 2048 history ids of one device, no owner is named more than 32 times; some owner exactly 32 times. `item_owner`: among the 128 samples of one device, no owner is named more than 2 times; some owner exactly 2 times. `hist_seg`: each row numbers 128 samples in order; each sample has 1 to 64 ids, one has exactly 64.
All inputs are finite; a program needn't handle non-finite values.
Results may differ from a plain program's by a relative error of at most 0.01.
The roundings to bfloat16 on the way count: a program that leaves them out, or rounds other values in their place, can miss the bound.
Values may be sent and summed in bfloat16 or wider, within the bound.
No kernel may reach another device: no remote copies, remote signals or barrier semaphores. Data moves between devices by JAX's collectives and lax.ppermute only.
A program may use at most 128 MiB of HBM per device.

v0:
```python
import jax
import jax.numpy as jnp
from jax import lax
from jax.sharding import PartitionSpec as P

EPS = 1e-06


def tower(x, weight):
    u = jnp.dot(x, weight, preferred_element_type=jnp.float32)
    r = lax.rsqrt(jnp.sum(u * u, -1, keepdims=True) + EPS)
    return (u * r, r)


def slot_rank(owner, devices):
    onehot = (owner[:, None] == jnp.arange(devices, dtype=jnp.int32)[None, :]).astype(jnp.int32)
    before = jnp.cumsum(onehot, 0) - onehot
    return jnp.sum(before * onehot, 1)


def lookup(table, wanted):
    rows_dev = table.shape[0]
    valid = wanted < rows_dev
    picked = table[jnp.minimum(wanted, rows_dev - 1)]
    return jnp.where(valid[..., None], picked, jnp.zeros_like(picked))


def local(
    user_table,
    item_table,
    hist_owner,
    hist_row,
    hist_seg,
    hist_wix,
    bag_weights,
    item_owner,
    item_row,
    user_proj,
    item_proj,
    logit_scale,
):
    rows_dev, width = user_table.shape
    n_dp = lax.axis_size("dp")
    n_tab = lax.axis_size("table")
    devices = n_dp * n_tab
    tokens = hist_row.shape[0]
    samples = item_row.shape[0]
    cap = max(2, 2 * tokens // devices)
    cap_item = max(2, 2 * samples // devices)
    myself = lax.axis_index(("dp", "table"))
    user_owner = hist_owner[:, 0]
    goods_owner = item_owner[:, 0]
    user_slot = slot_rank(user_owner, devices)
    goods_slot = slot_rank(goods_owner, devices)
    user_req = jnp.full((devices, cap), rows_dev, jnp.int32).at[user_owner, user_slot].set(hist_row)
    goods_req = (
        jnp.full((devices, cap_item), rows_dev, jnp.int32).at[goods_owner, goods_slot].set(item_row)
    )
    user_want, goods_want = (
        lax.all_to_all(user_req, ("dp", "table"), split_axis=0, concat_axis=0, tiled=True),
        lax.all_to_all(goods_req, ("dp", "table"), split_axis=0, concat_axis=0, tiled=True),
    )
    user_found = lookup(user_table, user_want)
    goods_found = lookup(item_table, goods_want)
    user_back, goods_back = (
        lax.all_to_all(user_found, ("dp", "table"), split_axis=0, concat_axis=0, tiled=True),
        lax.all_to_all(goods_found, ("dp", "table"), split_axis=0, concat_axis=0, tiled=True),
    )
    tok_rows = user_back[user_owner, user_slot]
    item_emb = goods_back[goods_owner, goods_slot]
    entries = bag_weights.shape[0]
    wts = jnp.sum(
        jnp.where(
            hist_wix[:, None] == jnp.arange(entries, dtype=jnp.int32)[None, :],
            bag_weights[None, :].astype(jnp.float32),
            0.0,
        ),
        1,
    ).astype(jnp.bfloat16)
    segment = hist_seg[0]
    member = segment[None, :] == jnp.arange(samples, dtype=jnp.int32)[:, None]
    coef = jnp.where(member, wts[None, :], jnp.zeros((), jnp.bfloat16))
    numer = jnp.dot(coef, tok_rows, preferred_element_type=jnp.float32)
    denom = jnp.sum(coef.astype(jnp.float32), 1)
    bag = (numer / denom[:, None]).astype(jnp.bfloat16)
    un, ru = tower(bag, user_proj)
    vn, rv = tower(item_emb, item_proj)
    uh = un.astype(jnp.bfloat16)
    vh = vn.astype(jnp.bfloat16)
    scale = logit_scale[0]
    vh_all = lax.all_gather(vh, ("dp", "table"), axis=0, tiled=True)
    total = vh_all.shape[0]
    mine = myself * samples + jnp.arange(samples, dtype=jnp.int32)
    scores = scale * jnp.dot(uh, vh_all.T, preferred_element_type=jnp.float32)
    top = jnp.max(scores, -1)
    expo = jnp.exp(scores - top[:, None])
    norm = jnp.sum(expo, -1)
    prob = expo / norm[:, None]
    hot = (jnp.arange(total, dtype=jnp.int32)[None, :] == mine[:, None]).astype(jnp.float32)
    pw = (prob - hot).astype(jnp.bfloat16)
    d_un = scale / total * jnp.dot(pw, vh_all, preferred_element_type=jnp.float32)
    terms = jnp.dot(pw.T, uh, preferred_element_type=jnp.float32)
    d_vsum = lax.psum_scatter(terms, ("dp", "table"), scatter_dimension=0, tiled=True)
    d_vn = scale / total * d_vsum
    d_u = ru * (d_un - un * jnp.sum(un * d_un, -1, keepdims=True))
    d_v = rv * (d_vn - vn * jnp.sum(vn * d_vn, -1, keepdims=True))
    highest = lax.Precision.HIGHEST
    user_part = jnp.dot(bag.astype(jnp.float32).T, d_u, precision=highest)
    goods_part = jnp.dot(item_emb.astype(jnp.float32).T, d_v, precision=highest)
    user_proj_grad, item_proj_grad = lax.psum((user_part, goods_part), ("dp", "table"))
    d_bag = jnp.dot(d_u, user_proj.astype(jnp.float32).T, precision=highest)
    g_tok = (wts.astype(jnp.float32) / denom[segment])[:, None] * d_bag[segment]
    user_send = jnp.zeros((devices, cap, width), jnp.float32).at[user_owner, user_slot].set(g_tok)
    goods_send = (
        jnp.zeros((devices, cap_item, width), jnp.float32).at[goods_owner, goods_slot].set(d_v)
    )
    user_got, goods_got = (
        lax.all_to_all(user_send, ("dp", "table"), split_axis=0, concat_axis=0, tiled=True),
        lax.all_to_all(goods_send, ("dp", "table"), split_axis=0, concat_axis=0, tiled=True),
    )
    user_grad = (
        jnp.zeros((rows_dev, width), jnp.float32)
        .at[user_want.reshape(-1)]
        .add(user_got.reshape(-1, width), mode="drop")
    )
    item_grad = (
        jnp.zeros((rows_dev, width), jnp.float32)
        .at[goods_want.reshape(-1)]
        .add(goods_got.reshape(-1, width), mode="drop")
    )
    return (user_grad, item_grad, user_proj_grad, item_proj_grad)


def solution(mesh):
    in_specs = (
        P(("dp", "table"), None),
        P(("dp", "table"), None),
        P(("dp", "table"), None),
        P(("dp", "table")),
        P(("dp", "table"), None),
        P(("dp", "table")),
        P(),
        P(("dp", "table"), None),
        P(("dp", "table")),
        P(),
        P(),
        P(),
    )
    out_specs = (P(("dp", "table"), None), P(("dp", "table"), None), P(), P())
    return jax.shard_map(local, mesh=mesh, in_specs=in_specs, out_specs=out_specs, check_vma=False)
```

profile of v0, /device:TPU:1, one launch (start us, length us, event | category | flops | bytes accessed | tf_op | source)
XLA Modules:
  0.0 1064.3 jit_solution(5642931868259348598)
XLA Ops:
  7.2 0.9 fusion.20
  8.3 0.8 select_reduce_fusion.1
  9.1 0.7 fusion.24
  9.8 11.0 %scatter_fusion = s32[128,2]{0,1:T(2,128)S(1)} fusion(s32[128,2]{0,1:T(2,128)S(1)} %broadcast.218, s32[128]{0:T(128)S(1)} %get-tuple-element.8, s32[128]{0:T(128)} %param.20), kind=kCustom, calls=%fused_computation.6 | custom fusion | bytes 2560 | tf_op jit(solution)/shard_map/scatter | solution.py:57
  20.9 21.1 %all_to_all.38 = s32[128,1,2]{2,1,0:T(1,128)S(1)} all-to-all(s32[128,1,2]{2,1,0:T(1,128)S(1)} %copy.51), channel_id=1, replica_groups=mesh['dp'=8,'table'=16] {'dp','table'}, dimensions={0} | all-to-all | bytes 2048 | tf_op jit(solution)/shard_map/all_to_all | solution.py:61
  42.0 0.5 broadcast.390
  42.5 0.8 fusion.31
  43.5 2.8 gather_fusion.3
  46.9 14.5 %all_to_all.39 = bf16[128,2,256]{2,1,0:T(2,128)(2,1)S(1)} all-to-all(bf16[128,2,256]{2,1,0:T(2,128)(2,1)S(1)} %broadcast_select_fusion.1), channel_id=1, replica_groups=mesh['dp'=8,'table'=16] {'dp','table'}, dimensions={0} | all-to-all | bytes 262144 | tf_op jit(solution)/shard_map/all_to_all | solution.py:67
  61.4 1.1 gather_fusion.4
  62.5 0.3 multiply_reduce_fusion.2
  62.8 0.7 multiply_convert_fusion
  63.6 0.3 fusion.12
  64.1 0.3 copy.47
  64.5 0.6 fusion.10
  65.4 8.2 scatter_custom_fusion.4
  73.7 13.6 %all_to_all.40 = s32[128,1,32]{2,1,0:T(1,128)S(1)} all-to-all(s32[128,1,32]{2,1,0:T(1,128)S(1)} %copy.48), channel_id=1, replica_groups=mesh['dp'=8,'table'=16] {'dp','table'}, dimensions={0} | all-to-all | bytes 32768 | tf_op jit(solution)/shard_map/all_to_all | solution.py:60
  87.3 0.8 broadcast_minimum_fusion.1
  88.5 17.0 %gather_fusion.1 = bf16[4096,256]{1,0:T(8,128)(2,1)} fusion(bf16[4096,256]{1,0:T(8,128)(2,1)S(1)} %copy-done, s32[4096]{0:T(1024)S(1)} %broadcast_clamp_fusion), kind=kCustom, calls=%fused_computation.1 | custom fusion | bytes 4210688 | tf_op jit(solution)/shard_map/gather | solution.py:24
  105.6 2.9 broadcast_select_fusion
  108.5 5.3 all-to-all-start.1
  115.1 35.3 %all-to-all-done.1 = bf16[128,32,256]{2,1,0:T(8,128)(2,1)} async-done(((bf16[128,32,256]{2,1,0:T(8,128)(2,1)}), bf16[128,32,256]{2,1,0:T(8,128)(2,1)}, u32[]{:S(2)}, u32[]{:S(2)}) %all-to-all-start.1) | async-done | bytes 2097184 | tf_op jit(solution)/shard_map/all_to_all | solution.py:66
  150.4 24.9 %gather_fusion.2 = bf16[2048,256]{1,0:T(8,128)(2,1)S(1)} fusion(bf16[128,32,256]{2,1,0:T(8,128)(2,1)} %all-to-all-done.1, s32[2048]{0:T(1024)S(1)} %bitcast.67), kind=kCustom, calls=%fused_computation.2 | custom fusion | bytes 2113536 | tf_op jit(solution)/shard_map/gather | solution.py:69
  175.3 0.3 fusion.8
  175.6 0.3 multiply_reduce_fusion.3
  175.9 6.3 fusion.32
  182.2 1.4 fusion
  183.6 2.3 subtract_convert_fusion
  185.9 2.0 copy-done.2
  187.9 8.1 fusion.27
  196.1 12.6 %gather_fusion = f32[2048]{0:T(1024)S(1)} fusion(f32[128]{0:T(128)S(1)} %convert_reduce_fusion, s32[2048]{0:T(1024)S(1)} %broadcast_clamp_fusion.1), kind=kCustom, calls=%fused_computation | custom fusion | bytes 24576 | tf_op jit(solution)/shard_map/gather | solution.py:112
  208.8 6.1 multiply_reduce_fusion.1
  214.8 0.3 fusion.29
  215.2 18.9 %scatter_custom_fusion.5 = f32[4096,256]{1,0:T(8,128)} fusion(s32[2048]{0:T(1024)S(1)} %get-tuple-element.17, f32[]{:T(128)} %constant.15.clone.1, f32[2048]{0:T(1024)S(1)} %convert_divide_fusion, f32[128,256]{1,0:T(8,128)S(1)} %fusion.29, s32[2048]{0:T(1024)S(1)} %broadcast_clamp_fusion.1), kind=kCustom, calls=%fused_computation.17 | custom fusion | flops 524288 | bytes 4341764
  234.1 5.2 all-to-all-start.4
  239.6 1.1 fusion.28
  240.7 616.9 %reduce-scatter.2.cloned.1.call-done = f32[128,256]{1,0:T(8,128)} async-done(((f32[16384,256]{1,0:T(8,128)}), f32[128,256]{1,0:T(8,128)}) %reduce-scatter.2.cloned.1.call-update) | async-done | bytes 131088 | tf_op jit(solution)/shard_map/reduce_scatter | solution.py:103
  857.6 1.1 multiply_reduce_fusion
  858.6 1.0 subtract_multiply_fusion
  859.7 0.8 broadcast_in_dim.57
  860.4 14.5 %scatter_fusion.1 = f32[128,2,256]{2,1,0:T(2,128)} fusion(f32[128,2,256]{2,1,0:T(2,128)} %broadcast_in_dim.57, s32[128]{0:T(128)S(1)} %get-tuple-element.8, f32[128,256]{1,0:T(8,128)S(1)} %subtract_multiply_fusion), kind=kCustom, calls=%fused_computation.8 | custom fusion | bytes 394240 | tf_op jit(solution)/shard_map/scatter | solution.py:115
  874.9 1.0 fusion.33
  875.9 39.3 %all-to-all-start.5 = ((f32[128,2,256]{2,1,0:T(2,128)}), f32[128,2,256]{2,1,0:T(2,128)S(1)}, u32[]{:S(2)}, u32[]{:S(2)}) async-start(f32[128,2,256]{2,1,0:T(2,128)} %scatter_fusion.1), calls=%async_computation.6 | async-start | bytes 524288 | tf_op jit(solution)/shard_map/all_to_all | solution.py:119
  915.3 25.2 %scatter_custom_fusion.1 = f32[4096,256]{1,0:T(8,128)} fusion(s32[4096]{0:T(1024)S(1)} %bitcast.80, f32[4096,256]{1,0:T(8,128)} %bitcast.26, f32[]{:T(128)} %constant.15.clone.1), kind=kCustom, calls=%fused_computation.22 | custom fusion | flops 1048576 | bytes 4194816 | tf_op jit(solution)/shard_map/scatter-add | solution.py:124
  940.7 4.2 scatter_custom_fusion.3
  944.9 109.5 %all-reduce.3.cloned.1.call-done = (f32[256,256]{1,0:T(8,128)}, f32[256,256]{1,0:T(8,128)}) async-done(((f32[256,256]{1,0:T(8,128)}, f32[256,256]{1,0:T(8,128)}), (f32[256,256]{1,0:T(8,128)}, f32[256,256]{1,0:T(8,128)})) %all-reduce.3.cloned.1.call-update) | async-done | bytes 524304 | tf_op jit(solution)/shard_map/psum | solution.py:110
  1054.4 1.7 copy.59
  1056.1 1.7 copy.60
  (73 shorter events, 3.1 us)
Async XLA Ops:
  7.2 81.3 %copy-start = (bf16[4096,256]{1,0:T(8,128)(2,1)S(1)}, bf16[4096,256]{1,0:T(8,128)(2,1)}, u32[]{:S(2)}) copy-start(bf16[4096,256]{1,0:T(8,128)(2,1)} %param.12) | copy-start | bytes 6291460
  7.2 55.3 %copy-start.4 = (bf16[256,256]{1,0:T(8,128)(2,1)S(1)}, bf16[256,256]{1,0:T(8,128)(2,1)}, u32[]{:S(2)}) copy-start(bf16[256,256]{1,0:T(8,128)(2,1)} %param.22) | copy-start | bytes 393220
  7.2 56.3 %copy-start.5 = (s32[2048,1]{0,1:T(1,128)S(1)}, s32[2048,1]{0,1:T(1,128)}, u32[]{:S(2)}) copy-start(s32[2048,1]{0,1:T(1,128)} %param.14) | copy-start | bytes 24580
  7.2 168.7 %all-gather.2.cloned.1.call-start = ((), (), s32[]{:S(2)}) async-start(), calls=%async_computation.7 | async-start | bytes 8454144 | tf_op jit(solution)/shard_map/all_gather | solution.py:91
  46.5 18.7 %copy-start.10 = (s32[2]{0:T(128)S(1)}, s32[2]{0:T(128)}, u32[]{:S(2)}) copy-start(s32[2]{0:T(128)} %constant.14) | copy-start | bytes 28
  46.5 18.8 %copy-start.8 = (s32[2]{0:T(128)S(1)}, s32[2]{0:T(128)}, u32[]{:S(2)}) copy-start(s32[2]{0:T(128)} %constant.11) | copy-start | bytes 28
  46.5 18.8 %copy-start.9 = (s32[2]{0:T(128)S(1)}, s32[2]{0:T(128)}, u32[]{:S(2)}) copy-start(s32[2]{0:T(128)} %constant.32) | copy-start | bytes 28
  105.6 8.5 copy-start.11
  105.6 9.1 copy-start.7
  105.6 9.3 copy-start.6
  108.5 41.9 %all-to-all-start.1 = ((bf16[128,32,256]{2,1,0:T(8,128)(2,1)}), bf16[128,32,256]{2,1,0:T(8,128)(2,1)}, u32[]{:S(2)}, u32[]{:S(2)}) async-start(bf16[128,32,256]{2,1,0:T(8,128)(2,1)} %broadcast_select_fusion), calls=%async_computation.1 | async-start | bytes 4194304 | tf_op jit(solution)/shard_map/all_to_all | solution.py:66
  113.8 743.8 %reduce-scatter.2.cloned.1.call-start = ((), (), s32[]{:S(2)}) async-start(), calls=%async_computation.8 | async-start | bytes 16908288 | tf_op jit(solution)/shard_map/reduce_scatter | solution.py:103
  150.4 25.2 %copy-start.3 = (bf16[256,256]{1,0:T(8,128)(2,1)S(1)}, bf16[256,256]{1,0:T(8,128)(2,1)}, u32[]{:S(2)}) copy-start(bf16[256,256]{1,0:T(8,128)(2,1)} %param.21) | copy-start | bytes 393220
  185.9 2.0 copy-start.2
  234.1 641.9 %all-to-all-start.4 = ((f32[128,32,256]{2,1,0:T(8,128)}), f32[128,32,256]{2,1,0:T(8,128)}, u32[]{:S(2)}, u32[]{:S(2)}) async-start(f32[128,32,256]{2,1,0:T(8,128)} %bitcast.68), calls=%async_computation.4 | async-start | bytes 8388608 | tf_op jit(solution)/shard_map/all_to_all | solution.py:118
  239.3 815.1 %all-reduce.3.cloned.1.call-start = ((), (), s32[]{:S(2)}) async-start(), calls=%async_computation.9 | async-start | bytes 1048576 | tf_op jit(solution)/shard_map/psum | solution.py:110
  875.9 64.6 %all-to-all-start.5 = ((f32[128,2,256]{2,1,0:T(2,128)}), f32[128,2,256]{2,1,0:T(2,128)S(1)}, u32[]{:S(2)}, u32[]{:S(2)}) async-start(f32[128,2,256]{2,1,0:T(2,128)} %scatter_fusion.1), calls=%async_computation.6 | async-start | bytes 524288 | tf_op jit(solution)/shard_map/all_to_all | solution.py:119
  915.3 142.4 %copy-start.1 = (bf16[4096,256]{1,0:T(8,128)(2,1)S(1)}, bf16[4096,256]{1,0:T(8,128)(2,1)}, u32[]{:S(2)}) copy-start(bf16[4096,256]{1,0:T(8,128)(2,1)} %param.12) | copy-start | bytes 6291460
Sparse Core Ops, SparseCore 0:
  63.7 81.1 all-gather.1
  196.2 661.2 reduce-scatter.1
  876.1 178.2 all-reduce.2
where the time goes:
time: 1070 us; the launch traced here: 1060 us
  waiting for transfers between devices  762 us (71%)
  local copies, waits for them, and re-layouts  101 us (9%)
  other arithmetic  64.1 us (6%)
  starting transfers between devices  50.1 us (5%)
  blocking collectives  49.2 us (5%)
  matrix products  23.7 us (2%)
  between operations  14.9 us (1%)
    reduce_scatter x1, waiting for transfers between devices, local(): lax.psum_scatter(terms, ('dp', 'table'), scatter_dimension=0, tiled=True)  617 us
    psum x1, waiting for transfers between devices, local(): lax.psum((user_part, goods_part), ('dp', 'table'))  109 us
    all_to_all x1, starting transfers between devices, local(): lax.all_to_all(goods_send, ('dp', 'table'), split_axis=0, concat_axis=0,...  39.3 us
    all_to_all x1, waiting for transfers between devices, local(): lax.all_to_all(user_found, ('dp', 'table'), split_axis=0, concat_axis=0,...  35.3 us
    scatter-add x1, other arithmetic, local(): user_grad = jnp.zeros((rows_dev, width), jnp.float32).at[user_want.reshap...  25.2 us
    gather x1, local copies, waits for them, and re-layouts, local(): tok_rows = user_back[user_owner, user_slot]  24.9 us
  transfers between devices with their start and end apart: 6, of which 3 were waited for; matrix products, arithmetic and copies ran while one was open for 14% of the time, Pallas kernels for 0%

commit v1 on v0

v1 whole, which is shorter than its diff:
```python
import jax
import jax.numpy as jnp
from jax import lax
from jax.sharding import PartitionSpec as P

EPS = 1e-06
AXES = ("dp", "table")


def tower(x, weight):
    u = jnp.dot(x, weight, preferred_element_type=jnp.float32)
    r = lax.rsqrt(jnp.sum(u * u, -1, keepdims=True) + EPS)
    return (u * r, r)


def slot_rank(owner, devices):
    onehot = (owner[:, None] == jnp.arange(devices, dtype=jnp.int32)[None, :]).astype(jnp.int32)
    before = jnp.cumsum(onehot, 0) - onehot
    return jnp.sum(before * onehot, 1)


def lookup(table, wanted):
    rows_dev = table.shape[0]
    valid = wanted < rows_dev
    picked = table[jnp.minimum(wanted, rows_dev - 1)]
    return jnp.where(valid[..., None], picked, jnp.zeros_like(picked))


def local(
    user_table,
    item_table,
    hist_owner,
    hist_row,
    hist_seg,
    hist_wix,
    bag_weights,
    item_owner,
    item_row,
    user_proj,
    item_proj,
    logit_scale,
):
    rows_dev, width = user_table.shape
    n_dp = lax.axis_size("dp")
    n_tab = lax.axis_size("table")
    devices = n_dp * n_tab
    tokens = hist_row.shape[0]
    samples = item_row.shape[0]
    cap = max(2, 2 * tokens // devices)
    cap_item = max(2, 2 * samples // devices)
    slots = cap + cap_item
    myself = lax.axis_index(AXES)
    user_owner = hist_owner[:, 0]
    goods_owner = item_owner[:, 0]
    user_slot = slot_rank(user_owner, devices)
    goods_slot = slot_rank(goods_owner, devices)
    user_key = user_owner * slots + user_slot
    goods_key = goods_owner * slots + cap + goods_slot
    keys = jnp.concatenate([user_key, goods_key])
    req = (
        jnp.full((devices * slots,), rows_dev, jnp.int32)
        .at[keys]
        .set(jnp.concatenate([hist_row, item_row]))
        .reshape(devices, slots)
    )
    want = lax.all_to_all(req, AXES, split_axis=0, concat_axis=0, tiled=True)
    user_want = want[:, :cap]
    goods_want = want[:, cap:]
    found = jnp.concatenate(
        [lookup(user_table, user_want), lookup(item_table, goods_want)], axis=1
    )
    back = lax.all_to_all(found, AXES, split_axis=0, concat_axis=0, tiled=True)
    got_rows = back.reshape(devices * slots, width)[keys]
    tok_rows = got_rows[:tokens]
    item_emb = got_rows[tokens:]
    entries = bag_weights.shape[0]
    wts = jnp.sum(
        jnp.where(
            hist_wix[:, None] == jnp.arange(entries, dtype=jnp.int32)[None, :],
            bag_weights[None, :].astype(jnp.float32),
            0.0,
        ),
        1,
    ).astype(jnp.bfloat16)
    segment = hist_seg[0]
    member = segment[None, :] == jnp.arange(samples, dtype=jnp.int32)[:, None]
    coef = jnp.where(member, wts[None, :], jnp.zeros((), jnp.bfloat16))
    numer = jnp.dot(coef, tok_rows, preferred_element_type=jnp.float32)
    denom = jnp.sum(coef.astype(jnp.float32), 1)
    bag = (numer / denom[:, None]).astype(jnp.bfloat16)
    un, ru = tower(bag, user_proj)
    vn, rv = tower(item_emb, item_proj)
    uh = un.astype(jnp.bfloat16)
    vh = vn.astype(jnp.bfloat16)
    scale = logit_scale[0]
    vh_all = lax.all_gather(vh, AXES, axis=0, tiled=True)
    uh_all = lax.all_gather(uh, AXES, axis=0, tiled=True)
    total = vh_all.shape[0]
    mine = myself * samples + jnp.arange(samples, dtype=jnp.int32)
    everyone = jnp.arange(total, dtype=jnp.int32)
    scores = scale * jnp.dot(uh, vh_all.T, preferred_element_type=jnp.float32)
    top = jnp.max(scores, -1)
    expo = jnp.exp(scores - top[:, None])
    norm = jnp.sum(expo, -1)
    stats_all = lax.all_gather(jnp.stack([top, norm], -1), AXES, axis=0, tiled=True)
    prob = expo / norm[:, None]
    hot = (everyone[None, :] == mine[:, None]).astype(jnp.float32)
    pw = (prob - hot).astype(jnp.bfloat16)
    d_un = scale / total * jnp.dot(pw, vh_all, preferred_element_type=jnp.float32)
    d_u = ru * (d_un - un * jnp.sum(un * d_un, -1, keepdims=True))
    highest = lax.Precision.HIGHEST
    user_part = jnp.dot(bag.astype(jnp.float32).T, d_u, precision=highest)
    d_bag = jnp.dot(d_u, user_proj.astype(jnp.float32).T, precision=highest)
    pick = jnp.concatenate([d_bag, denom[:, None]], axis=1)
    per_tok = jnp.dot(member.T.astype(jnp.float32), pick, precision=highest)
    g_tok = (wts.astype(jnp.float32) / per_tok[:, width])[:, None] * per_tok[:, :width]
    scores_c = scale * jnp.dot(vh, uh_all.T, preferred_element_type=jnp.float32)
    prob_c = jnp.exp(scores_c - stats_all[None, :, 0]) / stats_all[None, :, 1]
    hot_c = (everyone[None, :] == mine[:, None]).astype(jnp.float32)
    pw_c = (prob_c - hot_c).astype(jnp.bfloat16)
    d_vn = scale / total * jnp.dot(pw_c, uh_all, preferred_element_type=jnp.float32)
    d_v = rv * (d_vn - vn * jnp.sum(vn * d_vn, -1, keepdims=True))
    goods_part = jnp.dot(item_emb.astype(jnp.float32).T, d_v, precision=highest)
    user_proj_grad, item_proj_grad = lax.psum((user_part, goods_part), AXES)
    send = (
        jnp.zeros((devices * slots, width), jnp.float32)
        .at[keys]
        .set(jnp.concatenate([g_tok, d_v]))
        .reshape(devices, slots, width)
    )
    got = lax.all_to_all(send, AXES, split_axis=0, concat_axis=0, tiled=True)
    user_grad = (
        jnp.zeros((rows_dev, width), jnp.float32)
        .at[user_want.reshape(-1)]
        .add(got[:, :cap].reshape(-1, width), mode="drop")
    )
    item_grad = (
        jnp.zeros((rows_dev, width), jnp.float32)
        .at[goods_want.reshape(-1)]
        .add(got[:, cap:].reshape(-1, width), mode="drop")
    )
    return (user_grad, item_grad, user_proj_grad, item_proj_grad)


def solution(mesh):
    in_specs = (
        P(AXES, None),
        P(AXES, None),
        P(AXES, None),
        P(AXES),
        P(AXES, None),
        P(AXES),
        P(),
        P(AXES, None),
        P(AXES),
        P(),
        P(),
        P(),
    )
    out_specs = (P(AXES, None), P(AXES, None), P(), P())
    return jax.shard_map(local, mesh=mesh, in_specs=in_specs, out_specs=out_specs, check_vma=False)
```

time: 1070 us -> 500 us (0.47)
  waiting for transfers between devices: 762 us -> 256 us
  starting transfers between devices: 50.1 us -> 11.3 us
  local copies, waits for them, and re-layouts: 101 us -> 78.4 us
  blocking collectives: 49.2 us -> 70.4 us
  other arithmetic: 64.1 us -> 43.3 us
    reduce_scatter x1 -> x0, waiting for transfers between devices: 617 us -> none  [local(): lax.psum_scatter(terms, ('dp', 'table'), scatter_dimension=0, tiled=True)]
    all_gather x1 -> x2, waiting for transfers between devices: 0.02 us -> 70.7 us  [the longest x1 62.9 us: local(): vh_all = lax.all_gather(vh, AXES, axis=0, tiled=True)]
    all_to_all x3 -> x2, waiting for transfers between devices: 35.3 us -> 95 us  [the longest x1 60.5 us: local(): got = lax.all_to_all(send, AXES, split_axis=0, concat_axis=0, tiled=True)]
    all_gather x0 -> x1, blocking collectives: none -> 49.3 us  [local(): lax.all_gather(jnp.stack([top, norm], -1), AXES, axis=0, tiled=True)]
    all_to_all x3 -> x2, starting transfers between devices: 49.8 us -> 11 us  [the longest x1 5.78 us: local(): got = lax.all_to_all(send, AXES, split_axis=0, concat_axis=0, tiled=True)]
    gather x3 -> x1, local copies, waits for them, and re-layouts: 38.6 us -> 7.07 us  [local(): got_rows = back.reshape(devices * slots, width)[keys]]
    all_to_all x3 -> x1, blocking collectives: 49.2 us -> 21.1 us  [local(): want = lax.all_to_all(req, AXES, split_axis=0, concat_axis=0, tiled=True)]
    psum x1, waiting for transfers between devices: 109 us -> 90.2 us  [local(): user_proj_grad, item_proj_grad = lax.psum((user_part, goods_part), AXES)]
  transfers between devices with their start and end apart: 6 -> 5, of which waited for: 3 -> 5; matrix products, arithmetic and copies ran while one was open for 14% -> 11% of each run, Pallas kernels for 0% -> 0%
where the time goes in v1:
time: 500 us; the launch traced here: 499 us
  waiting for transfers between devices  256 us (51%)
  local copies, waits for them, and re-layouts  78.4 us (16%)
  blocking collectives  70.4 us (14%)
  other arithmetic  43.3 us (9%)
  matrix products  25 us (5%)
  between operations  15 us (3%)
  starting transfers between devices  11.3 us (2%)
    psum x1, waiting for transfers between devices, local(): user_proj_grad, item_proj_grad = lax.psum((user_part, goods_part), AXES)  90.2 us
    all_gather x1, waiting for transfers between devices, local(): vh_all = lax.all_gather(vh, AXES, axis=0, tiled=True)  62.9 us
    all_to_all x1, waiting for transfers between devices, local(): got = lax.all_to_all(send, AXES, split_axis=0, concat_axis=0, tiled=True)  60.5 us
    all_gather x1, blocking collectives, local(): lax.all_gather(jnp.stack([top, norm], -1), AXES, axis=0, tiled=True)  49.3 us
    all_to_all x1, waiting for transfers between devices, local(): back = lax.all_to_all(found, AXES, split_axis=0, concat_axis=0, tiled=True)  34.4 us
    scatter-add x1, other arithmetic, local(): user_grad = jnp.zeros((rows_dev, width), jnp.float32).at[user_want.reshap...  25.2 us
    all_to_all x1, blocking collectives, local(): want = lax.all_to_all(req, AXES, split_axis=0, concat_axis=0, tiled=True)  21.1 us
    gather x3, local copies, waits for them, and re-layouts, lookup(): picked = table[jnp.minimum(wanted, rows_dev - 1)]  19.9 us
  transfers between devices with their start and end apart: 5, of which 5 were waited for; matrix products, arithmetic and copies ran while one was open for 11% of the time, Pallas kernels for 0%

profile of v1, /device:TPU:1, one launch (start us, length us, event | category | flops | bytes accessed | tf_op | source)
XLA Modules:
  0.0 499.4 jit_solution(7406072734065943738)
XLA Ops:
  7.2 0.9 copy.30
  8.2 0.3 fusion.26
  8.6 0.3 copy.31
  9.0 0.6 fusion.23
  10.2 11.2 %scatter_custom_fusion = s32[4352]{0:T(1024)S(1)} fusion(s32[2176]{0:T(1024)S(1)} %fusion.44, s32[2176]{0:T(1024)S(1)} %pad_add_fusion, s32[]{:T(128)} %constant.17.clone.1), kind=kCustom, calls=%fused_computation.82 | custom fusion | bytes 17412 | tf_op jit(solution)/shard_map/scatter | solution.py:63
  21.5 21.1 %all_to_all.22 = s32[128,1,34]{2,1,0:T(1,128)S(1)} all-to-all(s32[128,1,34]{2,1,0:T(1,128)S(1)} %bitcast.52), channel_id=1, replica_groups=mesh['dp'=8,'table'=16] {'dp','table'}, dimensions={0} | all-to-all | bytes 34816 | tf_op jit(solution)/shard_map/all_to_all | solution.py:66
  42.6 0.6 compare_select_fusion.1
  43.2 0.7 fusion.50
  44.3 2.8 gather_fusion.1
  47.2 17.0 %gather_fusion = bf16[4096,256]{1,0:T(8,128)(2,1)} fusion(bf16[4096,256]{1,0:T(8,128)(2,1)S(1)} %copy-done, s32[4096]{0:T(1024)S(1)} %broadcast_clamp_fusion), kind=kCustom, calls=%fused_computation | custom fusion | bytes 4210688 | tf_op jit(solution)/shard_map/gather | solution.py:25
  64.2 1.9 broadcast_select_fusion
  66.4 1.8 pad_maximum_fusion
  68.2 5.2 %all-to-all-start.1 = ((bf16[128,34,256]{2,1,0:T(8,128)(2,1)}), bf16[128,34,256]{2,1,0:T(8,128)(2,1)}, u32[]{:S(2)}, u32[]{:S(2)}) async-start(bf16[128,34,256]{2,1,0:T(8,128)(2,1)} %pad_maximum_fusion), calls=%async_computation.1 | async-start | bytes 5242880 | tf_op jit(solution)/shard_map/all_to_all | solution.py:72
  73.5 34.4 %all-to-all-done.1 = bf16[128,34,256]{2,1,0:T(8,128)(2,1)} async-done(((bf16[128,34,256]{2,1,0:T(8,128)(2,1)}), bf16[128,34,256]{2,1,0:T(8,128)(2,1)}, u32[]{:S(2)}, u32[]{:S(2)}) %all-to-all-start.1) | async-done | bytes 2228256 | tf_op jit(solution)/shard_map/all_to_all | solution.py:72
  107.9 3.5 reshape.215
  111.4 7.1 %gather_fusion.2 = bf16[2176,256]{1,0:T(8,128)(2,1)S(1)} fusion(bf16[4352,256]{1,0:T(8,128)(2,1)S(1)} %reshape.215, s32[3072]{0:T(1024)S(1)} %pad_clamp_fusion), kind=kCustom, calls=%fused_computation.2 | custom fusion | bytes 2236928 | tf_op jit(solution)/shard_map/gather | solution.py:73
  118.5 0.3 multiply_reduce_fusion.2
  118.8 0.7 multiply_convert_fusion
  120.2 1.0 fusion.20
  121.2 1.2 multiply_reduce_fusion.3
  122.4 0.7 multiply_convert_fusion.1
  123.9 62.9 %all-gather.3.cloned.1.call-done = bf16[16384,256]{1,0:T(8,128)(2,1)} async-done(((bf16[128,256]{1,0:T(8,128)(2,1)}), bf16[16384,256]{1,0:T(8,128)(2,1)}) %all-gather.3.cloned.1.call-update) | async-done | bytes 8388624 | tf_op jit(solution)/shard_map/all_gather | solution.py:96
  186.9 6.3 %fusion.51 = (f32[128]{0:T(128)S(1)}, f32[128,16384]{1,0:T(8,128)S(1)}) fusion(bf16[128,256]{1,0:T(8,128)(2,1)} %multiply_convert_fusion.1, bf16[16384,256]{1,0:T(8,128)(2,1)} %all-gather.3.cloned.1.call-done, f32[]{:T(128)} %bitcast.44), kind=kOutput, calls=%fused_computation.102 | convolution fusion | flops 1077936000 | bytes 16843268 | tf_op jit(solution)/shard_map/dot_general | solution.py:101
  193.2 1.6 fusion.6
  194.8 49.3 %all_gather.11 = f32[16384,2]{0,1:T(2,128)S(1)} all-gather(f32[128,2]{0,1:T(2,128)S(1)} %pad_maximum_fusion.2), channel_id=1, replica_groups=mesh['dp'=8,'table'=16] {'dp','table'}, dimensions={0}, use_global_device_ids=true | all-gather | bytes 132096 | tf_op jit(solution)/shard_map/all_gather | solution.py:105
  244.1 2.9 multiply_reduce_fusion.1
  247.1 0.3 fusion.48
  247.4 1.1 fusion.24
  248.5 1.6 slice_multiply_fusion
  250.2 7.8 %all-gather.5.cloned.1.call-done = bf16[16384,256]{1,0:T(8,128)(2,1)} async-done(((bf16[128,256]{1,0:T(8,128)(2,1)}), bf16[16384,256]{1,0:T(8,128)(2,1)}) %all-gather.5.cloned.1.call-update) | async-done | bytes 8388624 | tf_op jit(solution)/shard_map/all_gather | solution.py:97
  258.0 9.9 %multiply_reduce_fusion = (f32[128]{0:T(128)S(1)}, f32[128,256]{1,0:T(8,128)S(1)}) fusion(f32[128,256]{1,0:T(8,128)S(1)} %get-tuple-element.15, f32[128]{0:T(128)S(1)} %add_rsqrt_fusion, bf16[16384,256]{1,0:T(8,128)(2,1)} %all-gather.5.cloned.1.call-done, bf16[128,256]{1,0:T(8,128)(2,1)S(1)} %copy-done.10, f32[16384]{0:T(1024)S(1)} %bitcast.56, ...), kind=kOutput, calls=%fused_computation.62 | convolution fusion | flops 2162294784 | bytes 8848904 | tf_op jit(solution)/shard_map/dot_general | solution.py:121
  268.0 0.6 copy-done.3
  268.6 0.8 copy.34
  269.4 1.8 pad_maximum_fusion.1
  271.2 1.9 copy.35
  273.1 15.7 %scatter_custom_fusion.1 = f32[4352,256]{1,0:T(8,128)} fusion(s32[2176]{0:T(1024)S(1)} %fusion.44, f32[2176,256]{1,0:T(8,128)} %copy.35, f32[]{:T(128)} %constant.16.clone.1), kind=kCustom, calls=%fused_computation.22 | custom fusion | bytes 4456960 | tf_op jit(solution)/shard_map/scatter | solution.py:128
  288.9 5.9 %reshape.216 = f32[128,34,256]{2,1,0:T(8,128)} reshape(f32[4352,256]{1,0:T(8,128)} %scatter_custom_fusion.1) | data formatting | bytes 8912896 | tf_op jit(solution)/shard_map/reshape | solution.py:129
  294.8 5.8 %all-to-all-start.2 = ((f32[128,34,256]{2,1,0:T(8,128)}), f32[128,34,256]{2,1,0:T(8,128)}, u32[]{:S(2)}, u32[]{:S(2)}) async-start(f32[128,34,256]{2,1,0:T(8,128)} %reshape.216), calls=%async_computation.2 | async-start | bytes 10485760 | tf_op jit(solution)/shard_map/all_to_all | solution.py:131
  300.7 1.0 fusion.38
  301.8 1.1 fusion.47
  303.0 60.5 %all-to-all-done.2 = f32[128,34,256]{2,1,0:T(8,128)} async-done(((f32[128,34,256]{2,1,0:T(8,128)}), f32[128,34,256]{2,1,0:T(8,128)}, u32[]{:S(2)}, u32[]{:S(2)}) %all-to-all-start.2) | async-done | bytes 4456480 | tf_op jit(solution)/shard_map/all_to_all | solution.py:131
  363.6 1.3 slice.65
  365.1 4.8 slice.64
  369.9 25.2 %scatter_custom_fusion.2 = f32[4096,256]{1,0:T(8,128)} fusion(s32[4096]{0:T(1024)S(1)} %bitcast.63, f32[4096,256]{1,0:T(8,128)} %bitcast.47, f32[]{:T(128)} %constant.16.clone.1), kind=kCustom, calls=%fused_computation.27 | custom fusion | flops 1048576 | bytes 4194816 | tf_op jit(solution)/shard_map/scatter-add | solution.py:135
  395.1 4.2 scatter_custom_fusion.3
  399.3 90.2 %all-reduce.3.cloned.1.call-done = (f32[256,256]{1,0:T(8,128)}, f32[256,256]{1,0:T(8,128)}) async-done(((f32[256,256]{1,0:T(8,128)}, f32[256,256]{1,0:T(8,128)}), (f32[256,256]{1,0:T(8,128)}, f32[256,256]{1,0:T(8,128)})) %all-reduce.3.cloned.1.call-update) | async-done | bytes 524304 | tf_op jit(solution)/shard_map/psum | solution.py:124
  489.5 1.7 copy.39
  491.2 1.7 copy.40
  (87 shorter events, 3.0 us)
Async XLA Ops:
  7.2 40.0 %copy-start = (bf16[4096,256]{1,0:T(8,128)(2,1)S(1)}, bf16[4096,256]{1,0:T(8,128)(2,1)}, u32[]{:S(2)}) copy-start(bf16[4096,256]{1,0:T(8,128)(2,1)} %param.12) | copy-start | bytes 6291460
  7.2 1.8 copy-start.12
  7.2 2.5 copy-start.17
  7.2 2.9 copy-start.16
  7.2 2.9 copy-start.20
  68.2 39.7 %all-to-all-start.1 = ((bf16[128,34,256]{2,1,0:T(8,128)(2,1)}), bf16[128,34,256]{2,1,0:T(8,128)(2,1)}, u32[]{:S(2)}, u32[]{:S(2)}) async-start(bf16[128,34,256]{2,1,0:T(8,128)(2,1)} %pad_maximum_fusion), calls=%async_computation.1 | async-start | bytes 5242880 | tf_op jit(solution)/shard_map/all_to_all | solution.py:72
  73.4 113.5 %all-gather.3.cloned.1.call-start = ((), (), s32[]{:S(2)}) async-start(), calls=%async_computation.3 | async-start | bytes 8454144 | tf_op jit(solution)/shard_map/all_gather | solution.py:96
  111.4 7.1 %copy-start.11 = (bf16[256,256]{1,0:T(8,128)(2,1)S(1)}, bf16[256,256]{1,0:T(8,128)(2,1)}, u32[]{:S(2)}) copy-start(bf16[256,256]{1,0:T(8,128)(2,1)} %param.22) | copy-start | bytes 393220
  111.4 8.4 %copy-start.21 = (bf16[64]{0:T(256)(128)(2,1)S(1)}, bf16[64]{0:T(256)(128)(2,1)}, u32[]{:S(2)}) copy-start(bf16[64]{0:T(256)(128)(2,1)} %param.18) | copy-start | bytes 388
  111.4 8.4 %copy-start.15 = (s32[2048]{0:T(1024)S(1)}, s32[2048]{0:T(1024)}, u32[]{:S(2)}) copy-start(s32[2048]{0:T(1024)} %param.17) | copy-start | bytes 24580
  111.4 8.6 %copy-start.13 = (s32[1,2048]{1,0:T(1,128)S(1)}, s32[1,2048]{1,0:T(1,128)}, u32[]{:S(2)}) copy-start(s32[1,2048]{1,0:T(1,128)} %param.16) | copy-start | bytes 24580
  119.6 138.4 %all-gather.5.cloned.1.call-start = ((), (), s32[]{:S(2)}) async-start(), calls=%async_computation.4 | async-start | bytes 8454144 | tf_op jit(solution)/shard_map/all_gather | solution.py:97
  193.2 50.9 %copy-start.2 = (bf16[16384,256]{1,0:T(8,128)(2,1)S(1)}, bf16[16384,256]{1,0:T(8,128)(2,1)}, u32[]{:S(2)}) copy-start(bf16[16384,256]{1,0:T(8,128)(2,1)} %all-gather.3.cloned.1.call-done) | copy-start | bytes 25165828
  244.1 3.0 copy-start.5
  244.1 3.3 copy-start.14
  247.1 3.0 copy-start.6
  247.1 10.9 %copy-start.18 = (f32[128]{0:T(128)}, f32[128]{0:T(128)S(1)}, u32[]{:S(2)}) copy-start(f32[128]{0:T(128)S(1)} %get-tuple-element.20) | copy-start | bytes 1540
  247.1 10.9 %copy-start.10 = (bf16[128,256]{1,0:T(8,128)(2,1)S(1)}, bf16[128,256]{1,0:T(8,128)(2,1)}, u32[]{:S(2)}) copy-start(bf16[128,256]{1,0:T(8,128)(2,1)} %multiply_convert_fusion) | copy-start | bytes 196612
  268.0 0.7 copy-start.3
  294.8 5.9 %copy-start.8 = (s32[128,32]{1,0:T(8,128)S(1)}, s32[128,32]{1,0:T(8,128)}, u32[]{:S(2)}) copy-start(s32[128,32]{1,0:T(8,128)} %get-tuple-element.11) | copy-start | bytes 49156
  294.8 6.0 %copy-start.4 = (f32[128,256]{1,0:T(8,128)S(1)}, f32[128,256]{1,0:T(8,128)}, u32[]{:S(2)}) copy-start(f32[128,256]{1,0:T(8,128)} %copy-done.3) | copy-start | bytes 393220
  294.8 7.0 %copy-start.7 = (f32[128,256]{1,0:T(8,128)S(1)}, f32[128,256]{1,0:T(8,128)}, u32[]{:S(2)}) copy-start(f32[128,256]{1,0:T(8,128)} %copy-done.6) | copy-start | bytes 393220
  294.8 7.0 %copy-start.19 = (f32[128]{0:T(128)S(1)}, f32[128]{0:T(128)}, u32[]{:S(2)}) copy-start(f32[128]{0:T(128)} %copy-done.18) | copy-start | bytes 1540
  294.8 8.1 %copy-start.9 = (s32[128,2]{1,0:T(8,128)S(1)}, s32[128,2]{1,0:T(8,128)}, u32[]{:S(2)}) copy-start(s32[128,2]{1,0:T(8,128)} %get-tuple-element.8) | copy-start | bytes 3076
  294.8 68.8 %all-to-all-start.2 = ((f32[128,34,256]{2,1,0:T(8,128)}), f32[128,34,256]{2,1,0:T(8,128)}, u32[]{:S(2)}, u32[]{:S(2)}) async-start(f32[128,34,256]{2,1,0:T(8,128)} %reshape.216), calls=%async_computation.2 | async-start | bytes 10485760 | tf_op jit(solution)/shard_map/all_to_all | solution.py:131
  300.6 188.9 %all-reduce.3.cloned.1.call-start = ((), (), s32[]{:S(2)}) async-start(), calls=%async_computation.5 | async-start | bytes 1048576 | tf_op jit(solution)/shard_map/psum | solution.py:124
  369.9 123.0 %copy-start.1 = (bf16[4096,256]{1,0:T(8,128)(2,1)S(1)}, bf16[4096,256]{1,0:T(8,128)(2,1)}, u32[]{:S(2)}) copy-start(bf16[4096,256]{1,0:T(8,128)(2,1)} %param.12) | copy-start | bytes 6291460
Sparse Core Ops, SparseCore 0:
  119.7 67.1 all-gather.2
  190.6 67.3 all-gather.4
  306.9 182.5 all-reduce.2

commit v2 on v1

--- a/solution.py
+++ b/solution.py
@@ -102,7 +102,10 @@
     top = jnp.max(scores, -1)
     expo = jnp.exp(scores - top[:, None])
     norm = jnp.sum(expo, -1)
-    stats_all = lax.all_gather(jnp.stack([top, norm], -1), AXES, axis=0, tiled=True)
+    stats = jnp.zeros((16, samples), jnp.float32).at[0].set(top).at[1].set(norm)
+    stats_all = lax.all_gather(stats, AXES, axis=0, tiled=True).reshape(devices, 16, samples)
+    top_all = stats_all[:, 0, :].reshape(total)
+    norm_all = stats_all[:, 1, :].reshape(total)
     prob = expo / norm[:, None]
     hot = (everyone[None, :] == mine[:, None]).astype(jnp.float32)
     pw = (prob - hot).astype(jnp.bfloat16)
@@ -115,20 +118,28 @@
     per_tok = jnp.dot(member.T.astype(jnp.float32), pick, precision=highest)
     g_tok = (wts.astype(jnp.float32) / per_tok[:, width])[:, None] * per_tok[:, :width]
     scores_c = scale * jnp.dot(vh, uh_all.T, preferred_element_type=jnp.float32)
-    prob_c = jnp.exp(scores_c - stats_all[None, :, 0]) / stats_all[None, :, 1]
+    prob_c = jnp.exp(scores_c - top_all[None, :]) / norm_all[None, :]
     hot_c = (everyone[None, :] == mine[:, None]).astype(jnp.float32)
     pw_c = (prob_c - hot_c).astype(jnp.bfloat16)
     d_vn = scale / total * jnp.dot(pw_c, uh_all, preferred_element_type=jnp.float32)
     d_v = rv * (d_vn - vn * jnp.sum(vn * d_vn, -1, keepdims=True))
     goods_part = jnp.dot(item_emb.astype(jnp.float32).T, d_v, precision=highest)
-    user_proj_grad, item_proj_grad = lax.psum((user_part, goods_part), AXES)
+    parts = jnp.stack([user_part, goods_part]).reshape(devices, -1, width)
+    chunk = parts.shape[1]
     send = (
         jnp.zeros((devices * slots, width), jnp.float32)
         .at[keys]
         .set(jnp.concatenate([g_tok, d_v]))
         .reshape(devices, slots, width)
     )
+    send = jnp.concatenate([send, parts], axis=1)
     got = lax.all_to_all(send, AXES, split_axis=0, concat_axis=0, tiled=True)
+    reduced = jnp.sum(got[:, slots:], 0)
+    padded = jnp.zeros((max(8, chunk), width), jnp.float32).at[:chunk].set(reduced)
+    gathered = lax.all_gather(padded, AXES, axis=0, tiled=True).reshape(devices, -1, width)
+    proj = gathered[:, :chunk].reshape(2, width, width)
+    user_proj_grad = proj[0]
+    item_proj_grad = proj[1]
     user_grad = (
         jnp.zeros((rows_dev, width), jnp.float32)
         .at[user_want.reshape(-1)]
@@ -137,7 +148,7 @@
     item_grad = (
         jnp.zeros((rows_dev, width), jnp.float32)
         .at[goods_want.reshape(-1)]
-        .add(got[:, cap:].reshape(-1, width), mode="drop")
+        .add(got[:, cap:slots].reshape(-1, width), mode="drop")
     )
     return (user_grad, item_grad, user_proj_grad, item_proj_grad)
 

time: 500 us -> 513 us (1.026)
  blocking collectives: 70.4 us -> 90.4 us
  waiting for transfers between devices: 256 us -> 239 us
  starting transfers between devices: 11.3 us -> 5.56 us
  matrix products: 25 us -> 30.4 us
    psum x1 -> x0, waiting for transfers between devices: 90.2 us -> none  [local(): user_proj_grad, item_proj_grad = lax.psum((user_part, goods_part), AXES)]
    all_gather x0 -> x2, waiting for transfers between devices: none -> 71.9 us  [the longest x1 47.9 us: local(): lax.all_gather(stats, AXES, axis=0, tiled=True)]
    all_to_all x0 -> x1, blocking collectives: none -> 69.3 us  [local(): got = lax.all_to_all(send, AXES, split_axis=0, concat_axis=0, tiled=True)]
    all_gather x1, waiting for transfers between devices: 7.78 us -> 69.6 us  [local(): uh_all = lax.all_gather(uh, AXES, axis=0, tiled=True)]
    all_to_all x1 -> x0, waiting for transfers between devices: 60.5 us -> none  [local(): got = lax.all_to_all(send, AXES, split_axis=0, concat_axis=0, tiled=True)]
    all_gather x1 -> x0, blocking collectives: 49.3 us -> none  [local(): lax.all_gather(jnp.stack([top, norm], -1), AXES, axis=0, tiled=True)]
    all_to_all x1 -> x0, starting transfers between devices: 5.78 us -> none  [local(): got = lax.all_to_all(send, AXES, split_axis=0, concat_axis=0, tiled=True)]
    dot_general x1, matrix products: 2.92 us -> 8.32 us  [local(): jnp.dot(pw, vh_all, preferred_element_type=jnp.float32)]
  transfers between devices with their start and end apart: 5 -> 5, of which waited for: 5 -> 5; matrix products, arithmetic and copies ran while one was open for 11% -> 10% of each run, Pallas kernels for 0% -> 0%
where the time goes in v2:
time: 513 us; the launch traced here: 512 us
  waiting for transfers between devices  239 us (47%)
  blocking collectives  90.4 us (18%)
  local copies, waits for them, and re-layouts  82.8 us (16%)
  other arithmetic  48.3 us (9%)
  matrix products  30.4 us (6%)
  between operations  15 us (3%)
  starting transfers between devices  5.56 us (1%)
    all_gather x1, waiting for transfers between devices, local(): uh_all = lax.all_gather(uh, AXES, axis=0, tiled=True)  69.6 us
    all_to_all x1, blocking collectives, local(): got = lax.all_to_all(send, AXES, split_axis=0, concat_axis=0, tiled=True)  69.3 us
    all_gather x1, waiting for transfers between devices, local(): vh_all = lax.all_gather(vh, AXES, axis=0, tiled=True)  63.3 us
    all_gather x1, waiting for transfers between devices, local(): lax.all_gather(stats, AXES, axis=0, tiled=True)  47.9 us
    all_to_all x1, waiting for transfers between devices, local(): back = lax.all_to_all(found, AXES, split_axis=0, concat_axis=0, tiled=True)  33.8 us
    scatter-add x1, other arithmetic, local(): user_grad = jnp.zeros((rows_dev, width), jnp.float32).at[user_want.reshap...  25.2 us
    all_gather x1, waiting for transfers between devices, local(): lax.all_gather(padded, AXES, axis=0, tiled=True).reshape(devices, -1, width)  23.9 us
    all_to_all x1, blocking collectives, local(): want = lax.all_to_all(req, AXES, split_axis=0, concat_axis=0, tiled=True)  21.1 us
  transfers between devices with their start and end apart: 5, of which 5 were waited for; matrix products, arithmetic and copies ran while one was open for 10% of the time, Pallas kernels for 0%

profile of v2, /device:TPU:1, one launch (start us, length us, event | category | flops | bytes accessed | tf_op | source)
XLA Modules:
  0.0 511.6 jit_solution(4389898350062893128)
XLA Ops:
  7.2 0.9 copy.30
  9.0 0.6 fusion.23
  10.2 11.2 %scatter_custom_fusion = s32[4352]{0:T(1024)S(1)} fusion(s32[2176]{0:T(1024)S(1)} %fusion.43, s32[2176]{0:T(1024)S(1)} %pad_add_fusion, s32[]{:T(128)} %constant.121.clone.1), kind=kCustom, calls=%fused_computation.86 | custom fusion | bytes 17412 | tf_op jit(solution)/shard_map/scatter | solution.py:63
  21.5 21.1 %all_to_all.22 = s32[128,1,34]{2,1,0:T(1,128)S(1)} all-to-all(s32[128,1,34]{2,1,0:T(1,128)S(1)} %bitcast.59), channel_id=1, replica_groups=mesh['dp'=8,'table'=16] {'dp','table'}, dimensions={0} | all-to-all | bytes 34816 | tf_op jit(solution)/shard_map/all_to_all | solution.py:66
  42.6 0.7 fusion.49
  43.7 2.8 gather_fusion.1
  46.6 17.0 %gather_fusion = bf16[4096,256]{1,0:T(8,128)(2,1)} fusion(bf16[4096,256]{1,0:T(8,128)(2,1)S(1)} %copy-done, s32[4096]{0:T(1024)S(1)} %broadcast_clamp_fusion), kind=kCustom, calls=%fused_computation | custom fusion | bytes 4210688 | tf_op jit(solution)/shard_map/gather | solution.py:25
  63.6 1.9 broadcast_select_fusion
  65.8 1.8 pad_maximum_fusion.1
  67.6 5.2 %all-to-all-start.1 = ((bf16[128,34,256]{2,1,0:T(8,128)(2,1)}), bf16[128,34,256]{2,1,0:T(8,128)(2,1)}, u32[]{:S(2)}, u32[]{:S(2)}) async-start(bf16[128,34,256]{2,1,0:T(8,128)(2,1)} %pad_maximum_fusion.1), calls=%async_computation.1 | async-start | bytes 5242880 | tf_op jit(solution)/shard_map/all_to_all | solution.py:72
  72.9 0.6 pad_clamp_fusion
  73.5 33.8 %all-to-all-done.1 = bf16[128,34,256]{2,1,0:T(8,128)(2,1)} async-done(((bf16[128,34,256]{2,1,0:T(8,128)(2,1)}), bf16[128,34,256]{2,1,0:T(8,128)(2,1)}, u32[]{:S(2)}, u32[]{:S(2)}) %all-to-all-start.1) | async-done | bytes 2228256 | tf_op jit(solution)/shard_map/all_to_all | solution.py:72
  107.3 3.5 reshape.305
  110.8 7.3 %gather_fusion.2 = bf16[2176,256]{1,0:T(8,128)(2,1)S(1)} fusion(bf16[4352,256]{1,0:T(8,128)(2,1)S(1)} %reshape.305, s32[3072]{0:T(1024)} %pad_clamp_fusion), kind=kCustom, calls=%fused_computation.2 | custom fusion | bytes 2236928 | tf_op jit(solution)/shard_map/gather | solution.py:73
  118.2 1.2 multiply_reduce_fusion.2
  119.4 0.7 multiply_convert_fusion
  121.0 0.9 select_reduce_fusion
  121.8 0.9 convert_reduce_fusion
  122.7 1.0 fusion.20
  124.1 63.3 %all-gather.5.cloned.1.call-done = bf16[16384,256]{1,0:T(8,128)(2,1)} async-done(((bf16[128,256]{1,0:T(8,128)(2,1)}), bf16[16384,256]{1,0:T(8,128)(2,1)}) %all-gather.5.cloned.1.call-update) | async-done | bytes 8388624 | tf_op jit(solution)/shard_map/all_gather | solution.py:96
  187.4 6.3 %fusion.50 = (f32[128]{0:T(128)S(1)}, f32[128,16384]{1,0:T(8,128)S(1)}) fusion(bf16[128,256]{1,0:T(8,128)(2,1)S(1)} %multiply_convert_fusion.1, bf16[16384,256]{1,0:T(8,128)(2,1)} %all-gather.5.cloned.1.call-done, f32[]{:T(128)} %bitcast.50), kind=kOutput, calls=%fused_computation.105 | convolution fusion | flops 1077936000 | bytes 16843268 | tf_op jit(solution)/shard_map/dot_general | solution.py:101
  193.7 3.2 copy-done.2
  196.9 1.6 fusion.6
  199.2 0.7 all-gather.7.cloned.1.call-update
  200.1 8.3 %multiply_reduce_fusion.1 = (f32[128]{0:T(128)S(1)}, f32[128,256]{1,0:T(8,128)S(1)}) fusion(f32[128,256]{1,0:T(8,128)S(1)} %get-tuple-element.49, f32[128]{0:T(128)S(1)} %add_rsqrt_fusion.1, bf16[16384,256]{1,0:T(8,128)(2,1)} %all-gather.5.cloned.1.call-done, f32[128,16384]{1,0:T(8,128)} %copy-done.2, s32[128]{0:T(128)S(1)} %iota_add_fusion, ...), kind=kOutput, calls=%fused_computation.69 | convolution fusion | flops 1086455680 | bytes 17041924 | tf_op jit(solution)/shard_map/dot_general | solution.py:112
  208.4 1.1 convolution_bitcast_fusion.1
  209.8 1.1 fusion.24
  210.9 1.6 slice_multiply_fusion
  212.5 47.9 %all-gather.9.cloned.1.call-done = f32[2048,128]{1,0:T(8,128)} async-done(((f32[16,128]{1,0:T(8,128)}), f32[2048,128]{1,0:T(8,128)}) %all-gather.9.cloned.1.call-update) | async-done | bytes 1048592 | tf_op jit(solution)/shard_map/all_gather | solution.py:106
  260.4 1.4 fusion.48
  261.8 69.6 %all-gather.7.cloned.1.call-done = bf16[16384,256]{1,0:T(8,128)(2,1)} async-done(((bf16[128,256]{1,0:T(8,128)(2,1)}), bf16[16384,256]{1,0:T(8,128)(2,1)}) %all-gather.7.cloned.1.call-update) | async-done | bytes 8388624 | tf_op jit(solution)/shard_map/all_gather | solution.py:97
  331.4 9.9 %multiply_reduce_fusion = (f32[128]{0:T(128)S(1)}, f32[128,256]{1,0:T(8,128)S(1)}) fusion(f32[128,256]{1,0:T(8,128)S(1)} %get-tuple-element.51, f32[128]{0:T(128)S(1)} %add_rsqrt_fusion, bf16[16384,256]{1,0:T(8,128)(2,1)} %all-gather.7.cloned.1.call-done, bf16[128,256]{1,0:T(8,128)(2,1)S(1)} %copy-done.8, f32[16384]{0:T(1024)S(1)} %bitcast.63, ...), kind=kOutput, calls=%fused_computation.67 | convolution fusion | flops 2162294784 | bytes 8848904 | tf_op jit(solution)/shard_map/dot_general | solution.py:124
  341.4 1.0 convolution_bitcast_fusion
  342.5 1.7 pad_maximum_fusion.2
  344.2 1.9 copy.35
  346.1 15.7 %scatter_custom_fusion.1 = f32[4352,256]{1,0:T(8,128)} fusion(s32[2176]{0:T(1024)S(1)} %fusion.43, f32[2176,256]{1,0:T(8,128)} %copy.35, f32[]{:T(128)} %constant.120.clone.1), kind=kCustom, calls=%fused_computation.23 | custom fusion | bytes 4456960 | tf_op jit(solution)/shard_map/scatter | solution.py:132
  361.9 6.0 %reshape.309 = f32[128,34,256]{2,1,0:T(8,128)} reshape(f32[4352,256]{1,0:T(8,128)} %scatter_custom_fusion.1) | data formatting | bytes 8912896 | tf_op jit(solution)/shard_map/reshape | solution.py:133
  368.0 2.9 pad_maximum_fusion
  371.0 69.3 %all_to_all.23 = f32[128,38,256]{2,1,0:T(8,128)} all-to-all(f32[128,38,256]{2,1,0:T(8,128)S(1)} %pad_maximum_fusion), channel_id=1, replica_groups=mesh['dp'=8,'table'=16] {'dp','table'}, dimensions={0} | all-to-all | bytes 9961472 | tf_op jit(solution)/shard_map/all_to_all | solution.py:136
  440.2 1.4 slice_reduce_fusion
  442.6 1.3 slice.127
  444.1 4.8 slice.126
  448.9 25.2 %scatter_custom_fusion.2 = f32[4096,256]{1,0:T(8,128)} fusion(s32[4096]{0:T(1024)S(1)} %bitcast.71, f32[4096,256]{1,0:T(8,128)} %bitcast.53, f32[]{:T(128)} %constant.120.clone.1), kind=kCustom, calls=%fused_computation.28 | custom fusion | flops 1048576 | bytes 4194816 | tf_op jit(solution)/shard_map/scatter-add | solution.py:146
  474.1 4.2 scatter_custom_fusion.3
  478.3 23.9 %all-gather.11.cloned.1.call-done = f32[1024,256]{1,0:T(8,128)} async-done(((f32[8,256]{1,0:T(8,128)}), f32[1024,256]{1,0:T(8,128)}) %all-gather.11.cloned.1.call-update) | async-done | bytes 1048592 | tf_op jit(solution)/shard_map/all_gather | solution.py:139
  502.2 1.3 fusion.47
  503.5 0.8 squeeze.19
  504.3 0.8 squeeze.20
  (83 shorter events, 5.4 us)
Async XLA Ops:
  7.2 39.4 %copy-start = (bf16[4096,256]{1,0:T(8,128)(2,1)S(1)}, bf16[4096,256]{1,0:T(8,128)(2,1)}, u32[]{:S(2)}) copy-start(bf16[4096,256]{1,0:T(8,128)(2,1)} %param.18) | copy-start | bytes 6291460
  7.2 1.8 copy-start.9
  7.2 2.5 copy-start.13
  7.2 2.9 copy-start.12
  7.2 2.9 copy-start.14
  67.6 39.7 %all-to-all-start.1 = ((bf16[128,34,256]{2,1,0:T(8,128)(2,1)}), bf16[128,34,256]{2,1,0:T(8,128)(2,1)}, u32[]{:S(2)}, u32[]{:S(2)}) async-start(bf16[128,34,256]{2,1,0:T(8,128)(2,1)} %pad_maximum_fusion.1), calls=%async_computation.1 | async-start | bytes 5242880 | tf_op jit(solution)/shard_map/all_to_all | solution.py:72
  72.8 114.6 %all-gather.5.cloned.1.call-start = ((), (), s32[]{:S(2)}) async-start(), calls=%async_computation.3 | async-start | bytes 8454144 | tf_op jit(solution)/shard_map/all_gather | solution.py:96
  110.8 9.5 %copy-start.15 = (bf16[64]{0:T(256)(128)(2,1)S(1)}, bf16[64]{0:T(256)(128)(2,1)}, u32[]{:S(2)}) copy-start(bf16[64]{0:T(256)(128)(2,1)} %param.24) | copy-start | bytes 388
  110.8 12.9 %copy-start.6 = (bf16[256,256]{1,0:T(8,128)(2,1)S(1)}, bf16[256,256]{1,0:T(8,128)(2,1)}, u32[]{:S(2)}) copy-start(bf16[256,256]{1,0:T(8,128)(2,1)} %param.27) | copy-start | bytes 393220
  120.1 140.3 %all-gather.9.cloned.1.call-start = ((), (), s32[]{:S(2)}) async-start(), calls=%async_computation.5 | async-start | bytes 1056768 | tf_op jit(solution)/shard_map/all_gather | solution.py:106
  124.1 69.6 %copy-start.5 = (bf16[128,256]{1,0:T(8,128)(2,1)}, bf16[128,256]{1,0:T(8,128)(2,1)S(1)}, u32[]{:S(2)}) copy-start(bf16[128,256]{1,0:T(8,128)(2,1)S(1)} %multiply_convert_fusion.1) | copy-start | bytes 196612
  193.7 3.2 copy-start.2
  198.5 0.6 copy-start.11
  199.2 132.2 %all-gather.7.cloned.1.call-start = ((), (), s32[]{:S(2)}) async-start(), calls=%async_computation.4 | async-start | bytes 8454144 | tf_op jit(solution)/shard_map/all_gather | solution.py:97
  199.9 302.3 %all-gather.11.cloned.1.call-start = ((), (), s32[]{:S(2)}) async-start(), calls=%async_computation.6 | async-start | bytes 1056768 | tf_op jit(solution)/shard_map/all_gather | solution.py:139
  200.1 9.7 %copy-start.10 = (s32[1,2048]{1,0:T(1,128)S(1)}, s32[1,2048]{1,0:T(1,128)}, u32[]{:S(2)}) copy-start(s32[1,2048]{1,0:T(1,128)} %param.22) | copy-start | bytes 24580
  208.4 122.9 %copy-start.8 = (bf16[128,256]{1,0:T(8,128)(2,1)S(1)}, bf16[128,256]{1,0:T(8,128)(2,1)}, u32[]{:S(2)}) copy-start(bf16[128,256]{1,0:T(8,128)(2,1)} %multiply_convert_fusion) | copy-start | bytes 196612
  361.9 6.0 %copy-start.3 = (f32[1,256,256]{2,1,0:T(8,128)S(1)}, f32[1,256,256]{2,1,0:T(8,128)}, u32[]{:S(2)}) copy-start(f32[1,256,256]{2,1,0:T(8,128)} %convolution_bitcast_fusion) | copy-start | bytes 786436
  361.9 6.0 %copy-start.4 = (f32[1,256,256]{2,1,0:T(8,128)S(1)}, f32[1,256,256]{2,1,0:T(8,128)}, u32[]{:S(2)}) copy-start(f32[1,256,256]{2,1,0:T(8,128)} %convolution_bitcast_fusion.1) | copy-start | bytes 786436
  371.0 71.4 %copy-start.7 = (s32[128,2]{1,0:T(8,128)S(1)}, s32[128,2]{1,0:T(8,128)}, u32[]{:S(2)}) copy-start(s32[128,2]{1,0:T(8,128)} %get-tuple-element.44) | copy-start | bytes 3076
  448.9 56.2 %copy-start.1 = (bf16[4096,256]{1,0:T(8,128)(2,1)S(1)}, bf16[4096,256]{1,0:T(8,128)(2,1)}, u32[]{:S(2)}) copy-start(bf16[4096,256]{1,0:T(8,128)(2,1)} %param.18) | copy-start | bytes 6291460
Sparse Core Ops, SparseCore 0:
  120.2 67.1 all-gather.4
  199.3 61.0 all-gather.8
  264.1 67.1 all-gather.6
  442.4 59.7 all-gather.10

commit v3 on v1

--- a/solution.py
+++ b/solution.py
@@ -93,8 +93,9 @@
     uh = un.astype(jnp.bfloat16)
     vh = vn.astype(jnp.bfloat16)
     scale = logit_scale[0]
-    vh_all = lax.all_gather(vh, AXES, axis=0, tiled=True)
-    uh_all = lax.all_gather(uh, AXES, axis=0, tiled=True)
+    both = lax.all_gather(jnp.stack([uh, vh]), AXES, axis=1, tiled=True)
+    uh_all = both[0]
+    vh_all = both[1]
     total = vh_all.shape[0]
     mine = myself * samples + jnp.arange(samples, dtype=jnp.int32)
     everyone = jnp.arange(total, dtype=jnp.int32)
@@ -102,7 +103,6 @@
     top = jnp.max(scores, -1)
     expo = jnp.exp(scores - top[:, None])
     norm = jnp.sum(expo, -1)
-    stats_all = lax.all_gather(jnp.stack([top, norm], -1), AXES, axis=0, tiled=True)
     prob = expo / norm[:, None]
     hot = (everyone[None, :] == mine[:, None]).astype(jnp.float32)
     pw = (prob - hot).astype(jnp.bfloat16)
@@ -114,21 +114,42 @@
     pick = jnp.concatenate([d_bag, denom[:, None]], axis=1)
     per_tok = jnp.dot(member.T.astype(jnp.float32), pick, precision=highest)
     g_tok = (wts.astype(jnp.float32) / per_tok[:, width])[:, None] * per_tok[:, :width]
+    stats = jnp.concatenate([top, norm]).reshape(1, 1, -1)
+    stats = jnp.broadcast_to(stats, (devices, 1, stats.shape[-1]))
+    user_parts = user_part.reshape(devices, -1, width)
+    stats = jnp.pad(stats, ((0, 0), (0, 0), (0, -stats.shape[-1] % width)))
+    stats = stats.reshape(devices, -1, width)
+    n_stat = stats.shape[1]
+    got_s = lax.all_to_all(
+        jnp.concatenate([stats, user_parts], axis=1), AXES, split_axis=0, concat_axis=0, tiled=True
+    )
+    flat_stats = got_s[:, :n_stat].reshape(devices, -1)
+    top_all = flat_stats[:, :samples].reshape(total)
+    norm_all = flat_stats[:, samples : 2 * samples].reshape(total)
+    user_red = jnp.sum(got_s[:, n_stat:], 0)
     scores_c = scale * jnp.dot(vh, uh_all.T, preferred_element_type=jnp.float32)
-    prob_c = jnp.exp(scores_c - stats_all[None, :, 0]) / stats_all[None, :, 1]
+    prob_c = jnp.exp(scores_c - top_all[None, :]) / norm_all[None, :]
     hot_c = (everyone[None, :] == mine[:, None]).astype(jnp.float32)
     pw_c = (prob_c - hot_c).astype(jnp.bfloat16)
     d_vn = scale / total * jnp.dot(pw_c, uh_all, preferred_element_type=jnp.float32)
     d_v = rv * (d_vn - vn * jnp.sum(vn * d_vn, -1, keepdims=True))
     goods_part = jnp.dot(item_emb.astype(jnp.float32).T, d_v, precision=highest)
-    user_proj_grad, item_proj_grad = lax.psum((user_part, goods_part), AXES)
+    goods_parts = goods_part.reshape(devices, -1, width)
+    chunk = goods_parts.shape[1]
     send = (
         jnp.zeros((devices * slots, width), jnp.float32)
         .at[keys]
         .set(jnp.concatenate([g_tok, d_v]))
         .reshape(devices, slots, width)
     )
+    send = jnp.concatenate([send, goods_parts], axis=1)
     got = lax.all_to_all(send, AXES, split_axis=0, concat_axis=0, tiled=True)
+    goods_red = jnp.sum(got[:, slots:], 0)
+    red = jnp.concatenate([user_red, goods_red])
+    padded = jnp.zeros((max(8, 2 * chunk), width), jnp.float32).at[: 2 * chunk].set(red)
+    gathered = lax.all_gather(padded, AXES, axis=0, tiled=True).reshape(devices, -1, width)
+    user_proj_grad = gathered[:, :chunk].reshape(width, width)
+    item_proj_grad = gathered[:, chunk : 2 * chunk].reshape(width, width)
     user_grad = (
         jnp.zeros((rows_dev, width), jnp.float32)
         .at[user_want.reshape(-1)]
@@ -137,7 +158,7 @@
     item_grad = (
         jnp.zeros((rows_dev, width), jnp.float32)
         .at[goods_want.reshape(-1)]
-        .add(got[:, cap:].reshape(-1, width), mode="drop")
+        .add(got[:, cap:slots].reshape(-1, width), mode="drop")
     )
     return (user_grad, item_grad, user_proj_grad, item_proj_grad)
 

time: 500 us -> 426 us (0.85)
  blocking collectives: 70.4 us -> 21.1 us
  waiting for transfers between devices: 256 us -> 214 us
  other arithmetic: 43.3 us -> 54.1 us
  starting transfers between devices: 11.3 us -> 18.3 us
    psum x1 -> x0, waiting for transfers between devices: 90.2 us -> none  [local(): user_proj_grad, item_proj_grad = lax.psum((user_part, goods_part), AXES)]
    all_gather x1 -> x0, blocking collectives: 49.3 us -> none  [local(): lax.all_gather(jnp.stack([top, norm], -1), AXES, axis=0, tiled=True)]
    all_gather x2, waiting for transfers between devices: 70.7 us -> 107 us  [the longest x1 77.4 us: local(): both = lax.all_gather(jnp.stack([uh, vh]), AXES, axis=1, tiled=True)]
    all_to_all x0 -> x1, waiting for transfers between devices: none -> 11.4 us  [local(): lax.all_to_all(jnp.concatenate([stats, user_parts], axis=1), AXES, split_...]
    all_to_all x0 -> x1, starting transfers between devices: none -> 7.35 us  [local(): lax.all_to_all(jnp.concatenate([stats, user_parts], axis=1), AXES, split_...]
    concatenate x0 -> x4, other arithmetic: none -> 6.94 us  [the longest x1 5.28 us: local(): send = jnp.concatenate([send, goods_parts], axis=1)]
  transfers between devices with their start and end apart: 5 -> 5, of which waited for: 5 -> 5; matrix products, arithmetic and copies ran while one was open for 11% -> 9% of each run, Pallas kernels for 0% -> 0%
where the time goes in v3:
time: 426 us; the launch traced here: 425 us
  waiting for transfers between devices  214 us (50%)
  local copies, waits for them, and re-layouts  76.5 us (18%)
  other arithmetic  54.1 us (13%)
  matrix products  26 us (6%)
  blocking collectives  21.1 us (5%)
  starting transfers between devices  18.3 us (4%)
  between operations  15.3 us (4%)
    all_gather x1, waiting for transfers between devices, local(): both = lax.all_gather(jnp.stack([uh, vh]), AXES, axis=1, tiled=True)  77.4 us
    all_to_all x1, waiting for transfers between devices, local(): got = lax.all_to_all(send, AXES, split_axis=0, concat_axis=0, tiled=True)  62.2 us
    all_to_all x1, waiting for transfers between devices, local(): back = lax.all_to_all(found, AXES, split_axis=0, concat_axis=0, tiled=True)  32.7 us
    all_gather x1, waiting for transfers between devices, local(): lax.all_gather(padded, AXES, axis=0, tiled=True).reshape(devices, -1, width)  29.9 us
    scatter-add x1, other arithmetic, local(): user_grad = jnp.zeros((rows_dev, width), jnp.float32).at[user_want.reshap...  25.2 us
    all_to_all x1, blocking collectives, local(): want = lax.all_to_all(req, AXES, split_axis=0, concat_axis=0, tiled=True)  21.1 us
    gather x3, local copies, waits for them, and re-layouts, lookup(): picked = table[jnp.minimum(wanted, rows_dev - 1)]  19.9 us
    scatter x1, local copies, waits for them, and re-layouts, local(): send = jnp.zeros((devices * slots, width), jnp.float32).at[keys].set(jnp....  15.7 us
  transfers between devices with their start and end apart: 5, of which 5 were waited for; matrix products, arithmetic and copies ran while one was open for 9% of the time, Pallas kernels for 0%

profile of v3, /device:TPU:1, one launch (start us, length us, event | category | flops | bytes accessed | tf_op | source)
XLA Modules:
  0.0 424.9 jit_solution(3097691100851666060)
XLA Ops:
  7.2 0.9 fusion.39
  8.3 0.8 select_reduce_fusion.1
  9.1 0.7 bitcast_add_fusion
  9.8 0.8 copy.30
  11.4 0.6 fusion.25
  12.1 11.2 %scatter_custom_fusion = s32[4352]{0:T(1024)S(1)} fusion(s32[2176]{0:T(1024)S(1)} %fusion.46, s32[2176]{0:T(1024)S(1)} %pad_add_fusion, s32[]{:T(128)} %constant.71.clone.1), kind=kCustom, calls=%fused_computation.94 | custom fusion | bytes 17412 | tf_op jit(solution)/shard_map/scatter | solution.py:63
  23.4 21.1 %all_to_all.27 = s32[128,1,34]{2,1,0:T(1,128)S(1)} all-to-all(s32[128,1,34]{2,1,0:T(1,128)S(1)} %bitcast.80), channel_id=1, replica_groups=mesh['dp'=8,'table'=16] {'dp','table'}, dimensions={0} | all-to-all | bytes 34816 | tf_op jit(solution)/shard_map/all_to_all | solution.py:66
  44.6 0.7 fusion.54
  45.5 2.8 gather_fusion.1
  48.8 17.0 %gather_fusion = bf16[4096,256]{1,0:T(8,128)(2,1)} fusion(bf16[4096,256]{1,0:T(8,128)(2,1)S(1)} %copy-done, s32[4096]{0:T(1024)S(1)} %broadcast_clamp_fusion), kind=kCustom, calls=%fused_computation | custom fusion | bytes 4210688 | tf_op jit(solution)/shard_map/gather | solution.py:25
  65.8 1.9 broadcast_select_fusion
  67.8 1.8 pad_maximum_fusion.1
  69.6 5.2 %all-to-all-start.1 = ((bf16[128,34,256]{2,1,0:T(8,128)(2,1)}), bf16[128,34,256]{2,1,0:T(8,128)(2,1)}, u32[]{:S(2)}, u32[]{:S(2)}) async-start(bf16[128,34,256]{2,1,0:T(8,128)(2,1)} %pad_maximum_fusion.1), calls=%async_computation.1 | async-start | bytes 5242880 | tf_op jit(solution)/shard_map/all_to_all | solution.py:72
  75.1 0.6 pad_clamp_fusion
  75.9 0.7 convert_reduce_fusion
  76.6 32.7 %all-to-all-done.1 = bf16[128,34,256]{2,1,0:T(8,128)(2,1)} async-done(((bf16[128,34,256]{2,1,0:T(8,128)(2,1)}), bf16[128,34,256]{2,1,0:T(8,128)(2,1)}, u32[]{:S(2)}, u32[]{:S(2)}) %all-to-all-start.1) | async-done | bytes 2228256 | tf_op jit(solution)/shard_map/all_to_all | solution.py:72
  109.3 3.5 reshape.263
  112.8 7.3 %gather_fusion.2 = bf16[2176,256]{1,0:T(8,128)(2,1)S(1)} fusion(bf16[4352,256]{1,0:T(8,128)(2,1)S(1)} %reshape.263, s32[3072]{0:T(1024)} %pad_clamp_fusion), kind=kCustom, calls=%fused_computation.2 | custom fusion | bytes 2236928 | tf_op jit(solution)/shard_map/gather | solution.py:73
  120.2 1.3 multiply_reduce_fusion.2
  121.5 1.0 fusion.22
  123.0 0.7 pad_maximum_fusion.4
  124.5 77.4 %all-gather.3.cloned.1.call-done = bf16[2,16384,256]{2,1,0:T(8,128)(2,1)} async-done(((bf16[2,128,256]{2,1,0:T(8,128)(2,1)}), bf16[2,16384,256]{2,1,0:T(8,128)(2,1)}) %all-gather.3.cloned.1.call-update) | async-done | bytes 16777232 | tf_op jit(solution)/shard_map/all_gather | solution.py:96
  201.8 5.3 %fusion.55 = (f32[128]{0:T(128)S(1)}, f32[128,16384]{1,0:T(8,128)S(1)}) fusion(bf16[2,16384,256]{2,1,0:T(8,128)(2,1)} %all-gather.3.cloned.1.call-done, f32[128,256]{1,0:T(8,128)S(1)} %get-tuple-element.29, f32[128]{0:T(128)S(1)} %add_rsqrt_fusion.1, f32[]{:T(128)} %bitcast.70), kind=kOutput, calls=%fused_computation.118 | convolution fusion | flops 1078001536 | bytes 16909824 | tf_op jit(solution)/shard_map/dot_general | solution.py:102
  207.2 1.6 fusion.6
  208.8 5.2 %multiply_reduce_fusion.1 = (f32[128]{0:T(128)S(1)}, f32[128,256]{1,0:T(8,128)S(1)}) fusion(f32[128,256]{1,0:T(8,128)S(1)} %get-tuple-element.29, f32[128]{0:T(128)S(1)} %add_rsqrt_fusion.1, bf16[2,16384,256]{2,1,0:T(8,128)(2,1)} %all-gather.3.cloned.1.call-done, f32[128,16384]{1,0:T(8,128)S(1)} %get-tuple-element.31, s32[128]{0:T(128)S(1)} %iota_add_fusion, ...), kind=kOutput, calls=%fused_computation.74 | convolution fusion | flops 1086455680 | bytes 17041924 | tf_op jit(solution)/shard_map/dot_general | solution.py:109
  214.9 1.0 pad_maximum_fusion.3
  215.9 7.4 %all-to-all-start.2 = ((f32[128,3,256]{2,1,0:T(4,128)}), f32[128,3,256]{2,1,0:T(4,128)S(1)}, u32[]{:S(2)}, u32[]{:S(2)}) async-start(f32[128,3,256]{2,1,0:T(4,128)} %pad_maximum_fusion.3), calls=%async_computation.2 | async-start | bytes 1048576 | tf_op jit(solution)/shard_map/all_to_all | solution.py:123
  223.3 1.1 fusion.26
  224.4 1.6 slice_multiply_fusion
  225.9 11.4 %all-to-all-done.2 = f32[128,3,256]{2,1,0:T(4,128)S(1)} async-done(((f32[128,3,256]{2,1,0:T(4,128)}), f32[128,3,256]{2,1,0:T(4,128)S(1)}, u32[]{:S(2)}, u32[]{:S(2)}) %all-to-all-start.2) | async-done | bytes 393248 | tf_op jit(solution)/shard_map/all_to_all | solution.py:123
  237.5 10.1 %multiply_reduce_fusion = (f32[128]{0:T(128)S(1)}, f32[128,256]{1,0:T(8,128)S(1)}) fusion(f32[128,256]{1,0:T(8,128)S(1)} %get-tuple-element.27, f32[128]{0:T(128)S(1)} %add_rsqrt_fusion, bf16[2,16384,256]{2,1,0:T(8,128)(2,1)} %all-gather.3.cloned.1.call-done, f32[16384]{0:T(1024)S(1)} %get-tuple-element.21, f32[16384]{0:T(1024)S(1)} %get-tuple-element.20, ...), kind=kOutput, calls=%fused_computation.72 | convolution fusion | flops 2162360320 | bytes 17303560 | tf_op jit(solution)/shard_map/dot_general | solution.py:134
  247.6 1.2 fusion.40
  249.0 1.8 pad_maximum_fusion.2
  250.8 1.9 copy.35
  252.7 15.7 %scatter_custom_fusion.1 = f32[4352,256]{1,0:T(8,128)} fusion(s32[2176]{0:T(1024)S(1)} %fusion.46, f32[2176,256]{1,0:T(8,128)} %copy.35, f32[]{:T(128)} %constant.70.clone.1), kind=kCustom, calls=%fused_computation.28 | custom fusion | bytes 4456960 | tf_op jit(solution)/shard_map/scatter | solution.py:142
  268.4 5.9 %reshape.266 = f32[128,34,256]{2,1,0:T(8,128)} reshape(f32[4352,256]{1,0:T(8,128)} %scatter_custom_fusion.1) | data formatting | bytes 8912896 | tf_op jit(solution)/shard_map/reshape | solution.py:143
  274.3 5.3 %pad_maximum_fusion = f32[128,36,256]{2,1,0:T(8,128)} fusion(f32[128,2,256]{2,1,0:T(2,128)S(1)} %reshape.267, f32[128,34,256]{2,1,0:T(8,128)} %reshape.266), kind=kLoop, calls=%fused_computation.23 | loop fusion | flops 1179648 | bytes 9437184 | tf_op jit(solution)/shard_map/concatenate | solution.py:145
  279.6 5.2 %all-to-all-start.3 = ((f32[128,36,256]{2,1,0:T(8,128)}), f32[128,36,256]{2,1,0:T(8,128)}, u32[]{:S(2)}, u32[]{:S(2)}) async-start(f32[128,36,256]{2,1,0:T(8,128)} %pad_maximum_fusion), calls=%async_computation.3 | async-start | bytes 10485760 | tf_op jit(solution)/shard_map/all_to_all | solution.py:146
  285.4 62.2 %all-to-all-done.3 = f32[128,36,256]{2,1,0:T(8,128)} async-done(((f32[128,36,256]{2,1,0:T(8,128)}), f32[128,36,256]{2,1,0:T(8,128)}, u32[]{:S(2)}, u32[]{:S(2)}) %all-to-all-start.3) | async-done | bytes 4718624 | tf_op jit(solution)/shard_map/all_to_all | solution.py:146
  347.5 1.8 slice_reduce_fusion
  349.4 0.6 select_maximum_fusion
  350.5 4.8 %slice.111 = f32[128,32,256]{2,1,0:T(8,128)} slice(f32[128,36,256]{2,1,0:T(8,128)} %all-to-all-done.3), slice={[0:128], [0:32], [0:256]} | slice | bytes 8388608 | tf_op jit(solution)/shard_map/slice | solution.py:156
  355.3 25.2 %scatter_custom_fusion.2 = f32[4096,256]{1,0:T(8,128)} fusion(s32[4096]{0:T(1024)S(1)} %bitcast.89, f32[4096,256]{1,0:T(8,128)} %bitcast.73, f32[]{:T(128)} %constant.70.clone.1), kind=kCustom, calls=%fused_computation.33 | custom fusion | flops 1048576 | bytes 4194816 | tf_op jit(solution)/shard_map/scatter-add | solution.py:156
  380.5 4.2 scatter_custom_fusion.3
  384.7 29.9 %all-gather.5.cloned.1.call-done = f32[1024,256]{1,0:T(8,128)} async-done(((f32[8,256]{1,0:T(8,128)}), f32[1024,256]{1,0:T(8,128)}) %all-gather.5.cloned.1.call-update) | async-done | bytes 1048592 | tf_op jit(solution)/shard_map/all_gather | solution.py:150
  414.6 1.8 fusion.53
  416.3 0.9 reshape.272
  417.2 0.9 reshape.273
  (77 shorter events, 5.1 us)
Async XLA Ops:
  7.2 41.6 %copy-start = (bf16[4096,256]{1,0:T(8,128)(2,1)S(1)}, bf16[4096,256]{1,0:T(8,128)(2,1)}, u32[]{:S(2)}) copy-start(bf16[4096,256]{1,0:T(8,128)(2,1)} %param.14) | copy-start | bytes 6291460
  7.2 4.2 copy-start.5
  7.2 4.9 %copy-start.11 = (s32[128]{0:T(128)S(1)}, s32[128]{0:T(128)}, u32[]{:S(2)}) copy-start(s32[128]{0:T(128)} %param.22) | copy-start | bytes 1540
  7.2 4.9 %copy-start.9 = (s32[2048]{0:T(1024)S(1)}, s32[2048]{0:T(1024)}, u32[]{:S(2)}) copy-start(s32[2048]{0:T(1024)} %param.17) | copy-start | bytes 24580
  67.8 7.3 %copy-start.12 = (bf16[64]{0:T(256)(128)(2,1)S(1)}, bf16[64]{0:T(256)(128)(2,1)}, u32[]{:S(2)}) copy-start(bf16[64]{0:T(256)(128)(2,1)} %param.20) | copy-start | bytes 388
  67.8 7.9 %copy-start.8 = (s32[2048]{0:T(1024)S(1)}, s32[2048]{0:T(1024)}, u32[]{:S(2)}) copy-start(s32[2048]{0:T(1024)} %param.19) | copy-start | bytes 24580
  67.8 8.1 %copy-start.6 = (s32[1,2048]{1,0:T(1,128)S(1)}, s32[1,2048]{1,0:T(1,128)}, u32[]{:S(2)}) copy-start(s32[1,2048]{1,0:T(1,128)} %param.18) | copy-start | bytes 24580
  69.6 39.7 %all-to-all-start.1 = ((bf16[128,34,256]{2,1,0:T(8,128)(2,1)}), bf16[128,34,256]{2,1,0:T(8,128)(2,1)}, u32[]{:S(2)}, u32[]{:S(2)}) async-start(bf16[128,34,256]{2,1,0:T(8,128)(2,1)} %pad_maximum_fusion.1), calls=%async_computation.1 | async-start | bytes 5242880 | tf_op jit(solution)/shard_map/all_to_all | solution.py:72
  74.8 127.0 %all-gather.3.cloned.1.call-start = ((), (), s32[]{:S(2)}) async-start(), calls=%async_computation.4 | async-start | bytes 16908288 | tf_op jit(solution)/shard_map/all_gather | solution.py:96
  112.8 9.7 %copy-start.3 = (bf16[256,256]{1,0:T(8,128)(2,1)S(1)}, bf16[256,256]{1,0:T(8,128)(2,1)}, u32[]{:S(2)}) copy-start(bf16[256,256]{1,0:T(8,128)(2,1)} %param.23) | copy-start | bytes 393220
  120.2 87.0 %copy-start.2 = (bf16[2176,256]{1,0:T(8,128)(2,1)}, bf16[2176,256]{1,0:T(8,128)(2,1)S(1)}, u32[]{:S(2)}) copy-start(bf16[2176,256]{1,0:T(8,128)(2,1)S(1)} %gather_fusion.2) | copy-start | bytes 3342340
  120.2 4.1 copy-start.10
  208.8 14.5 %copy-start.7 = (s32[1,2048]{1,0:T(1,128)S(1)}, s32[1,2048]{1,0:T(1,128)}, u32[]{:S(2)}) copy-start(s32[1,2048]{1,0:T(1,128)} %param.18) | copy-start | bytes 24580
  215.9 21.4 %all-to-all-start.2 = ((f32[128,3,256]{2,1,0:T(4,128)}), f32[128,3,256]{2,1,0:T(4,128)S(1)}, u32[]{:S(2)}, u32[]{:S(2)}) async-start(f32[128,3,256]{2,1,0:T(4,128)} %pad_maximum_fusion.3), calls=%async_computation.2 | async-start | bytes 1048576 | tf_op jit(solution)/shard_map/all_to_all | solution.py:123
  279.6 70.5 %copy-start.4 = (s32[128,2]{1,0:T(8,128)S(1)}, s32[128,2]{1,0:T(8,128)}, u32[]{:S(2)}) copy-start(s32[128,2]{1,0:T(8,128)} %get-tuple-element.22) | copy-start | bytes 3076
  279.6 67.9 %all-to-all-start.3 = ((f32[128,36,256]{2,1,0:T(8,128)}), f32[128,36,256]{2,1,0:T(8,128)}, u32[]{:S(2)}, u32[]{:S(2)}) async-start(f32[128,36,256]{2,1,0:T(8,128)} %pad_maximum_fusion), calls=%async_computation.3 | async-start | bytes 10485760 | tf_op jit(solution)/shard_map/all_to_all | solution.py:146
  284.9 129.7 %all-gather.5.cloned.1.call-start = ((), (), s32[]{:S(2)}) async-start(), calls=%async_computation.5 | async-start | bytes 1056768 | tf_op jit(solution)/shard_map/all_gather | solution.py:150
  355.3 62.8 %copy-start.1 = (bf16[4096,256]{1,0:T(8,128)(2,1)S(1)}, bf16[4096,256]{1,0:T(8,128)(2,1)}, u32[]{:S(2)}) copy-start(bf16[4096,256]{1,0:T(8,128)(2,1)} %param.14) | copy-start | bytes 6291460
Sparse Core Ops, SparseCore 0:
  123.8 78.0 all-gather.2
  350.1 64.3 all-gather.4

commit v4 on v3

--- a/solution.py
+++ b/solution.py
@@ -57,12 +57,22 @@
     user_key = user_owner * slots + user_slot
     goods_key = goods_owner * slots + cap + goods_slot
     keys = jnp.concatenate([user_key, goods_key])
-    req = (
-        jnp.full((devices * slots,), rows_dev, jnp.int32)
-        .at[keys]
-        .set(jnp.concatenate([hist_row, item_row]))
-        .reshape(devices, slots)
+    entries = bag_weights.shape[0]
+    segment = hist_seg[0]
+    row_bits = max(1, (rows_dev - 1).bit_length())
+    seg_bits = max(1, (samples - 1).bit_length())
+    packed = jnp.concatenate(
+        [
+            hist_row | (segment << row_bits) | (hist_wix << (row_bits + seg_bits)),
+            item_row | (jnp.arange(samples, dtype=jnp.int32) << row_bits),
+        ]
     )
+    info = jnp.full((devices * slots,), -1, jnp.int32).at[keys].set(packed)
+    filled = info >= 0
+    req = jnp.where(filled, info & ((1 << row_bits) - 1), rows_dev).reshape(devices, slots)
+    slot_seg = (info >> row_bits) & ((1 << seg_bits) - 1)
+    slot_wix = info >> (row_bits + seg_bits)
+    is_user = (jnp.arange(devices * slots, dtype=jnp.int32) % slots) < cap
     want = lax.all_to_all(req, AXES, split_axis=0, concat_axis=0, tiled=True)
     user_want = want[:, :cap]
     goods_want = want[:, cap:]
@@ -70,24 +80,24 @@
         [lookup(user_table, user_want), lookup(item_table, goods_want)], axis=1
     )
     back = lax.all_to_all(found, AXES, split_axis=0, concat_axis=0, tiled=True)
-    got_rows = back.reshape(devices * slots, width)[keys]
-    tok_rows = got_rows[:tokens]
-    item_emb = got_rows[tokens:]
-    entries = bag_weights.shape[0]
+    back = back.reshape(devices * slots, width)
     wts = jnp.sum(
         jnp.where(
-            hist_wix[:, None] == jnp.arange(entries, dtype=jnp.int32)[None, :],
+            slot_wix[:, None] == jnp.arange(entries, dtype=jnp.int32)[None, :],
             bag_weights[None, :].astype(jnp.float32),
             0.0,
         ),
         1,
     ).astype(jnp.bfloat16)
-    segment = hist_seg[0]
-    member = segment[None, :] == jnp.arange(samples, dtype=jnp.int32)[:, None]
+    sample_ids = jnp.arange(samples, dtype=jnp.int32)
+    of_sample = filled[None, :] & (slot_seg[None, :] == sample_ids[:, None])
+    member = of_sample & is_user[None, :]
     coef = jnp.where(member, wts[None, :], jnp.zeros((), jnp.bfloat16))
-    numer = jnp.dot(coef, tok_rows, preferred_element_type=jnp.float32)
+    numer = jnp.dot(coef, back, preferred_element_type=jnp.float32)
     denom = jnp.sum(coef.astype(jnp.float32), 1)
     bag = (numer / denom[:, None]).astype(jnp.bfloat16)
+    item_pick = (of_sample & ~is_user[None, :]).astype(jnp.bfloat16)
+    item_emb = jnp.dot(item_pick, back, preferred_element_type=jnp.float32).astype(jnp.bfloat16)
     un, ru = tower(bag, user_proj)
     vn, rv = tower(item_emb, item_proj)
     uh = un.astype(jnp.bfloat16)
@@ -111,9 +121,6 @@
     highest = lax.Precision.HIGHEST
     user_part = jnp.dot(bag.astype(jnp.float32).T, d_u, precision=highest)
     d_bag = jnp.dot(d_u, user_proj.astype(jnp.float32).T, precision=highest)
-    pick = jnp.concatenate([d_bag, denom[:, None]], axis=1)
-    per_tok = jnp.dot(member.T.astype(jnp.float32), pick, precision=highest)
-    g_tok = (wts.astype(jnp.float32) / per_tok[:, width])[:, None] * per_tok[:, :width]
     stats = jnp.concatenate([top, norm]).reshape(1, 1, -1)
     stats = jnp.broadcast_to(stats, (devices, 1, stats.shape[-1]))
     user_parts = user_part.reshape(devices, -1, width)
@@ -134,17 +141,21 @@
     d_vn = scale / total * jnp.dot(pw_c, uh_all, preferred_element_type=jnp.float32)
     d_v = rv * (d_vn - vn * jnp.sum(vn * d_vn, -1, keepdims=True))
     goods_part = jnp.dot(item_emb.astype(jnp.float32).T, d_v, precision=highest)
+    pick = jnp.concatenate([d_bag, d_v, denom[:, None]], axis=1)
+    per_slot = jnp.dot(of_sample.T.astype(jnp.float32), pick, precision=highest)
+    g_slot = (wts.astype(jnp.float32) / per_slot[:, 2 * width])[:, None] * per_slot[:, :width]
+    g_slot = jnp.where(is_user[:, None], g_slot, per_slot[:, width : 2 * width])
+    g_slot = jnp.where(filled[:, None], g_slot, 0.0)
     goods_parts = goods_part.reshape(devices, -1, width)
     chunk = goods_parts.shape[1]
-    send = (
-        jnp.zeros((devices * slots, width), jnp.float32)
-        .at[keys]
-        .set(jnp.concatenate([g_tok, d_v]))
-        .reshape(devices, slots, width)
+    hi = goods_parts.astype(jnp.bfloat16)
+    lo = (goods_parts - hi.astype(jnp.float32)).astype(jnp.bfloat16)
+    send = jnp.concatenate(
+        [g_slot.astype(jnp.bfloat16).reshape(devices, slots, width), hi, lo], axis=1
     )
-    send = jnp.concatenate([send, goods_parts], axis=1)
     got = lax.all_to_all(send, AXES, split_axis=0, concat_axis=0, tiled=True)
-    goods_red = jnp.sum(got[:, slots:], 0)
+    tail = got[:, slots:].astype(jnp.float32)
+    goods_red = jnp.sum(tail[:, :chunk] + tail[:, chunk:], 0)
     red = jnp.concatenate([user_red, goods_red])
     padded = jnp.zeros((max(8, 2 * chunk), width), jnp.float32).at[: 2 * chunk].set(red)
     gathered = lax.all_gather(padded, AXES, axis=0, tiled=True).reshape(devices, -1, width)
@@ -153,12 +164,12 @@
     user_grad = (
         jnp.zeros((rows_dev, width), jnp.float32)
         .at[user_want.reshape(-1)]
-        .add(got[:, :cap].reshape(-1, width), mode="drop")
+        .add(got[:, :cap].reshape(-1, width).astype(jnp.float32), mode="drop")
     )
     item_grad = (
         jnp.zeros((rows_dev, width), jnp.float32)
         .at[goods_want.reshape(-1)]
-        .add(got[:, cap:slots].reshape(-1, width), mode="drop")
+        .add(got[:, cap:slots].reshape(-1, width).astype(jnp.float32), mode="drop")
     )
     return (user_grad, item_grad, user_proj_grad, item_proj_grad)
 

time: 426 us -> 366 us (0.86)
  local copies, waits for them, and re-layouts: 76.5 us -> 46.7 us
  waiting for transfers between devices: 214 us -> 191 us
  other arithmetic: 54.1 us -> 44.5 us
  matrix products: 26 us -> 30.3 us
    all_to_all x1, waiting for transfers between devices: 62.2 us -> 34.3 us  [local(): got = lax.all_to_all(send, AXES, split_axis=0, concat_axis=0, tiled=True)]
    scatter x2 -> x1, local copies, waits for them, and re-layouts: 26.9 us -> 11.2 us  [local(): info = jnp.full((devices * slots,), -1, jnp.int32).at[keys].set(packed)]
    gather x1 -> x0, local copies, waits for them, and re-layouts: 7.33 us -> none  [local(): got_rows = back.reshape(devices * slots, width)[keys]]
    dot_general x2 -> x3, matrix products: 2.07 us -> 8.25 us  [the longest x1 3.81 us: local(): per_slot = jnp.dot(of_sample.T.astype(jnp.float32), pick, precision=highest)]
    concatenate x3 -> x2, other arithmetic: 7.04 us -> 2.11 us  [the longest x1 2.11 us: local(): jnp.concatenate([g_slot.astype(jnp.bfloat16).reshape(devices, slots, widt...]
    reshape x3 -> x2, local copies, waits for them, and re-layouts: 9.59 us -> 5.52 us  [the longest x1 3.41 us: local(): g_slot.astype(jnp.bfloat16).reshape(devices, slots, width)]
where the time goes in v4:
time: 366 us; the launch traced here: 365 us
  waiting for transfers between devices  191 us (52%)
  local copies, waits for them, and re-layouts  46.7 us (13%)
  other arithmetic  44.5 us (12%)
  matrix products  30.3 us (8%)
  blocking collectives  21.1 us (6%)
  starting transfers between devices  16.3 us (4%)
  between operations  15.3 us (4%)
    all_gather x1, waiting for transfers between devices, local(): both = lax.all_gather(jnp.stack([uh, vh]), AXES, axis=1, tiled=True)  77.5 us
    all_to_all x1, waiting for transfers between devices, local(): got = lax.all_to_all(send, AXES, split_axis=0, concat_axis=0, tiled=True)  34.3 us
    all_to_all x1, waiting for transfers between devices, local(): back = lax.all_to_all(found, AXES, split_axis=0, concat_axis=0, tiled=True)  33.5 us
    all_gather x1, waiting for transfers between devices, local(): lax.all_gather(padded, AXES, axis=0, tiled=True).reshape(devices, -1, width)  31.6 us
    scatter-add x1, other arithmetic, local(): user_grad = jnp.zeros((rows_dev, width), jnp.float32).at[user_want.reshap...  23.3 us
    all_to_all x1, blocking collectives, local(): want = lax.all_to_all(req, AXES, split_axis=0, concat_axis=0, tiled=True)  21.1 us
    gather x3, local copies, waits for them, and re-layouts, lookup(): picked = table[jnp.minimum(wanted, rows_dev - 1)]  19.9 us
    all_to_all x1, waiting for transfers between devices, local(): lax.all_to_all(jnp.concatenate([stats, user_parts], axis=1), AXES, split_...  13.6 us
  transfers between devices with their start and end apart: 5, of which 5 were waited for; matrix products, arithmetic and copies ran while one was open for 9% of the time, Pallas kernels for 0%

profile of v4, /device:TPU:1, one launch (start us, length us, event | category | flops | bytes accessed | tf_op | source)
XLA Modules:
  0.0 364.8 jit_solution(12898185724270823278)
XLA Ops:
  7.2 0.9 fusion.63
  8.3 0.8 select_reduce_fusion.1
  9.1 0.7 bitcast_add_fusion
  9.8 0.8 copy.31
  10.6 0.3 fusion.52
  11.1 0.3 copy.32
  11.4 0.6 fusion.51
  12.2 11.2 %scatter_custom_fusion = s32[4352]{0:T(1024)S(1)} fusion(s32[2176]{0:T(1024)S(1)} %fusion.71, s32[2176]{0:T(1024)S(1)} %pad_add_fusion, s32[]{:T(128)} %constant.42.clone.1), kind=kCustom, calls=%fused_computation.117 | custom fusion | bytes 17412 | tf_op jit(solution)/shard_map/scatter | solution.py:70
  23.5 21.1 %all_to_all.27 = s32[128,1,34]{2,1,0:T(1,128)S(1)} all-to-all(s32[128,1,34]{2,1,0:T(1,128)S(1)} %bitcast.83), channel_id=1, replica_groups=mesh['dp'=8,'table'=16] {'dp','table'}, dimensions={0} | all-to-all | bytes 34816 | tf_op jit(solution)/shard_map/all_to_all | solution.py:76
  44.7 0.7 fusion.80
  45.6 2.8 gather_fusion.1
  48.9 17.0 %gather_fusion = bf16[4096,256]{1,0:T(8,128)(2,1)} fusion(bf16[4096,256]{1,0:T(8,128)(2,1)S(1)} %copy-done, s32[4096]{0:T(1024)S(1)} %broadcast_clamp_fusion), kind=kCustom, calls=%fused_computation | custom fusion | bytes 4210688 | tf_op jit(solution)/shard_map/gather | solution.py:25
  65.9 1.9 broadcast_select_fusion
  67.9 1.8 pad_maximum_fusion
  69.7 4.3 %all-to-all-start.1 = ((bf16[128,34,256]{2,1,0:T(8,128)(2,1)}), bf16[128,34,256]{2,1,0:T(8,128)(2,1)S(1)}, u32[]{:S(2)}, u32[]{:S(2)}) async-start(bf16[128,34,256]{2,1,0:T(8,128)(2,1)} %pad_maximum_fusion), calls=%async_computation.1 | async-start | bytes 5242880 | tf_op jit(solution)/shard_map/all_to_all | solution.py:82
  74.5 0.6 convert_reduce_fusion
  75.1 33.5 %all-to-all-done.1 = bf16[128,34,256]{2,1,0:T(8,128)(2,1)S(1)} async-done(((bf16[128,34,256]{2,1,0:T(8,128)(2,1)}), bf16[128,34,256]{2,1,0:T(8,128)(2,1)S(1)}, u32[]{:S(2)}, u32[]{:S(2)}) %all-to-all-start.1) | async-done | bytes 2228256 | tf_op jit(solution)/shard_map/all_to_all | solution.py:82
  108.7 2.1 reshape.292
  110.8 2.3 fusion.33
  113.3 2.2 fusion.47
  116.0 0.7 pad_maximum_fusion.3
  117.3 77.5 %all-gather.3.cloned.1.call-done = bf16[2,16384,256]{2,1,0:T(8,128)(2,1)} async-done(((bf16[2,128,256]{2,1,0:T(8,128)(2,1)}), bf16[2,16384,256]{2,1,0:T(8,128)(2,1)}) %all-gather.3.cloned.1.call-update) | async-done | bytes 16777232 | tf_op jit(solution)/shard_map/all_gather | solution.py:106
  194.9 5.3 %fusion.81 = (f32[128]{0:T(128)S(1)}, f32[128,16384]{1,0:T(8,128)S(1)}) fusion(bf16[2,16384,256]{2,1,0:T(8,128)(2,1)} %all-gather.3.cloned.1.call-done, f32[128,256]{1,0:T(8,128)S(1)} %get-tuple-element.32, f32[128]{0:T(128)S(1)} %add_rsqrt_fusion.1, f32[]{:T(128)} %bitcast.73), kind=kOutput, calls=%fused_computation.144 | convolution fusion | flops 1078001536 | bytes 16909824 | tf_op jit(solution)/shard_map/dot_general | solution.py:112
  200.2 1.6 fusion.6
  201.8 5.2 %multiply_reduce_fusion.1 = (f32[128]{0:T(128)S(1)}, f32[128,256]{1,0:T(8,128)S(1)}) fusion(f32[128,256]{1,0:T(8,128)S(1)} %get-tuple-element.32, f32[128]{0:T(128)S(1)} %add_rsqrt_fusion.1, bf16[2,16384,256]{2,1,0:T(8,128)(2,1)} %all-gather.3.cloned.1.call-done, f32[128,16384]{1,0:T(8,128)S(1)} %get-tuple-element.34, s32[128]{0:T(128)S(1)} %iota_add_fusion, ...), kind=kOutput, calls=%fused_computation.90 | convolution fusion | flops 1086455680 | bytes 17041924 | tf_op jit(solution)/shard_map/dot_general | solution.py:119
  207.0 0.4 fusion.77
  207.6 1.0 pad_maximum_fusion.2
  208.6 7.4 %all-to-all-start.2 = ((f32[128,3,256]{2,1,0:T(4,128)}), f32[128,3,256]{2,1,0:T(4,128)S(1)}, u32[]{:S(2)}, u32[]{:S(2)}) async-start(f32[128,3,256]{2,1,0:T(4,128)} %pad_maximum_fusion.2), calls=%async_computation.2 | async-start | bytes 1048576 | tf_op jit(solution)/shard_map/all_to_all | solution.py:130
  216.1 0.3 fusion.78
  216.4 13.6 %all-to-all-done.2 = f32[128,3,256]{2,1,0:T(4,128)S(1)} async-done(((f32[128,3,256]{2,1,0:T(4,128)}), f32[128,3,256]{2,1,0:T(4,128)S(1)}, u32[]{:S(2)}, u32[]{:S(2)}) %all-to-all-start.2) | async-done | bytes 393248 | tf_op jit(solution)/shard_map/all_to_all | solution.py:130
  230.1 10.0 %multiply_reduce_fusion = (f32[128]{0:T(128)S(1)}, f32[128,256]{1,0:T(8,128)S(1)}) fusion(f32[128,256]{1,0:T(8,128)S(1)} %get-tuple-element.30, f32[128]{0:T(128)S(1)} %add_rsqrt_fusion, bf16[2,16384,256]{2,1,0:T(8,128)(2,1)} %all-gather.3.cloned.1.call-done, f32[16384]{0:T(1024)S(1)} %get-tuple-element.21, f32[16384]{0:T(1024)S(1)} %get-tuple-element.20, ...), kind=kOutput, calls=%fused_computation.88 | convolution fusion | flops 2162360320 | bytes 17303560 | tf_op jit(solution)/shard_map/dot_general | solution.py:141
  240.3 0.3 fusion.82
  240.9 3.8 %fusion.17 = f32[4352,513]{0,1:T(8,128)S(1)} fusion(s32[4352]{0:T(1024)S(1)} %get-tuple-element.27, pred[4352]{0:T(1024)(128)(4,1)S(1)} %get-tuple-element.39, f32[128,1]{1,0:T(8,128)S(1)} %copy.34, f32[128,256]{1,0:T(8,128)S(1)} %subtract_multiply_fusion, f32[128,256]{1,0:T(8,128)S(1)} %fusion.78), kind=kOutput, calls=%fused_computation.34 | convolution fusion | flops 3430482176 | bytes 9214720 | tf_op jit(solution)/shard_map/dot_general | solution.py:145
  244.8 0.6 fusion.10
  245.4 2.4 copy.35
  247.8 3.4 reshape.295
  251.2 2.1 pad_maximum_fusion.1
  253.4 4.2 %all-to-all-start.3 = ((bf16[128,38,256]{2,1,0:T(8,128)(2,1)}), bf16[128,38,256]{2,1,0:T(8,128)(2,1)S(1)}, u32[]{:S(2)}, u32[]{:S(2)}) async-start(bf16[128,38,256]{2,1,0:T(8,128)(2,1)} %pad_maximum_fusion.1), calls=%async_computation.3 | async-start | bytes 5242880 | tf_op jit(solution)/shard_map/all_to_all | solution.py:156
  257.5 0.3 all-gather.5.cloned.1.call-start
  258.1 34.3 %all-to-all-done.3 = bf16[128,38,256]{2,1,0:T(8,128)(2,1)S(1)} async-done(((bf16[128,38,256]{2,1,0:T(8,128)(2,1)}), bf16[128,38,256]{2,1,0:T(8,128)(2,1)S(1)}, u32[]{:S(2)}, u32[]{:S(2)}) %all-to-all-start.3) | async-done | bytes 2490400 | tf_op jit(solution)/shard_map/all_to_all | solution.py:156
  292.6 0.6 select_maximum_fusion
  293.8 1.6 slice.112
  295.5 23.3 %scatter_custom_fusion.1 = f32[4096,256]{1,0:T(8,128)} fusion(s32[4096]{0:T(1024)S(1)} %bitcast.88, bf16[4096,256]{1,0:T(8,128)(2,1)} %bitcast.76, f32[]{:T(128)} %constant.41.clone.1), kind=kCustom, calls=%fused_computation.25 | custom fusion | flops 2097152 | bytes 6291460 | tf_op jit(solution)/shard_map/scatter-add | solution.py:167
  318.7 4.2 %scatter_custom_fusion.2 = f32[4096,256]{1,0:T(8,128)} fusion(s32[256]{0:T(256)S(1)} %bitcast.92, f32[256,256]{1,0:T(8,128)S(1)} %reshape.340, f32[]{:T(128)} %constant.41.clone.1), kind=kCustom, calls=%fused_computation.39 | custom fusion | flops 65536 | bytes 4194308 | tf_op jit(solution)/shard_map/scatter-add | solution.py:172
  322.9 31.6 %all-gather.5.cloned.1.call-done = f32[1024,256]{1,0:T(8,128)} async-done(((f32[8,256]{1,0:T(8,128)}), f32[1024,256]{1,0:T(8,128)}) %all-gather.5.cloned.1.call-update) | async-done | bytes 1048592 | tf_op jit(solution)/shard_map/all_gather | solution.py:161
  354.5 1.7 fusion.79
  356.2 0.9 reshape.299
  357.1 0.9 reshape.300
  (79 shorter events, 4.4 us)
Async XLA Ops:
  7.2 41.7 %copy-start = (bf16[4096,256]{1,0:T(8,128)(2,1)S(1)}, bf16[4096,256]{1,0:T(8,128)(2,1)}, u32[]{:S(2)}) copy-start(bf16[4096,256]{1,0:T(8,128)(2,1)} %param.14) | copy-start | bytes 6291460
  7.2 4.2 %copy-start.5 = (s32[2048,1]{0,1:T(1,128)S(1)}, s32[2048,1]{0,1:T(1,128)}, u32[]{:S(2)}) copy-start(s32[2048,1]{0,1:T(1,128)} %param.16) | copy-start | bytes 24580
  7.2 4.9 %copy-start.9 = (s32[128]{0:T(128)S(1)}, s32[128]{0:T(128)}, u32[]{:S(2)}) copy-start(s32[128]{0:T(128)} %param.22) | copy-start | bytes 1540
  7.2 4.9 %copy-start.6 = (s32[1,2048]{1,0:T(1,128)S(1)}, s32[1,2048]{1,0:T(1,128)}, u32[]{:S(2)}) copy-start(s32[1,2048]{1,0:T(1,128)} %param.18) | copy-start | bytes 24580
  7.2 4.9 %copy-start.7 = (s32[2048]{0:T(1024)S(1)}, s32[2048]{0:T(1024)}, u32[]{:S(2)}) copy-start(s32[2048]{0:T(1024)} %param.19) | copy-start | bytes 24580
  7.2 4.9 %copy-start.8 = (s32[2048]{0:T(1024)S(1)}, s32[2048]{0:T(1024)}, u32[]{:S(2)}) copy-start(s32[2048]{0:T(1024)} %param.17) | copy-start | bytes 24580
  67.9 6.3 %copy-start.10 = (bf16[64]{0:T(256)(128)(2,1)S(1)}, bf16[64]{0:T(256)(128)(2,1)}, u32[]{:S(2)}) copy-start(bf16[64]{0:T(256)(128)(2,1)} %param.20) | copy-start | bytes 388
  69.7 39.0 %all-to-all-start.1 = ((bf16[128,34,256]{2,1,0:T(8,128)(2,1)}), bf16[128,34,256]{2,1,0:T(8,128)(2,1)S(1)}, u32[]{:S(2)}, u32[]{:S(2)}) async-start(bf16[128,34,256]{2,1,0:T(8,128)(2,1)} %pad_maximum_fusion), calls=%async_computation.1 | async-start | bytes 5242880 | tf_op jit(solution)/shard_map/all_to_all | solution.py:82
  74.0 120.9 %all-gather.3.cloned.1.call-start = ((), (), s32[]{:S(2)}) async-start(), calls=%async_computation.4 | async-start | bytes 16908288 | tf_op jit(solution)/shard_map/all_gather | solution.py:106
  75.1 37.9 %copy-start.4 = (bf16[256,256]{1,0:T(8,128)(2,1)S(1)}, bf16[256,256]{1,0:T(8,128)(2,1)}, u32[]{:S(2)}) copy-start(bf16[256,256]{1,0:T(8,128)(2,1)} %param.24) | copy-start | bytes 393220
  110.8 4.7 %copy-start.2 = (bf16[256,256]{1,0:T(8,128)(2,1)S(1)}, bf16[256,256]{1,0:T(8,128)(2,1)}, u32[]{:S(2)}) copy-start(bf16[256,256]{1,0:T(8,128)(2,1)} %param.23) | copy-start | bytes 393220
  208.6 21.4 %all-to-all-start.2 = ((f32[128,3,256]{2,1,0:T(4,128)}), f32[128,3,256]{2,1,0:T(4,128)S(1)}, u32[]{:S(2)}, u32[]{:S(2)}) async-start(f32[128,3,256]{2,1,0:T(4,128)} %pad_maximum_fusion.2), calls=%async_computation.2 | async-start | bytes 1048576 | tf_op jit(solution)/shard_map/all_to_all | solution.py:130
  253.4 40.0 %copy-start.3 = (s32[128,2]{1,0:T(8,128)S(1)}, s32[128,2]{1,0:T(8,128)}, u32[]{:S(2)}) copy-start(s32[128,2]{1,0:T(8,128)} %get-tuple-element.22) | copy-start | bytes 3076
  253.4 39.0 %all-to-all-start.3 = ((bf16[128,38,256]{2,1,0:T(8,128)(2,1)}), bf16[128,38,256]{2,1,0:T(8,128)(2,1)S(1)}, u32[]{:S(2)}, u32[]{:S(2)}) async-start(bf16[128,38,256]{2,1,0:T(8,128)(2,1)} %pad_maximum_fusion.1), calls=%async_computation.3 | async-start | bytes 5242880 | tf_op jit(solution)/shard_map/all_to_all | solution.py:156
  257.5 97.0 %all-gather.5.cloned.1.call-start = ((), (), s32[]{:S(2)}) async-start(), calls=%async_computation.5 | async-start | bytes 1056768 | tf_op jit(solution)/shard_map/all_gather | solution.py:161
  295.4 62.6 %copy-start.1 = (bf16[4096,256]{1,0:T(8,128)(2,1)S(1)}, bf16[4096,256]{1,0:T(8,128)(2,1)}, u32[]{:S(2)}) copy-start(bf16[4096,256]{1,0:T(8,128)(2,1)} %param.14) | copy-start | bytes 6291460
Sparse Core Ops, SparseCore 0:
  116.8 78.0 all-gather.2
  293.4 61.0 all-gather.4

commit v5 on v4

--- a/solution.py
+++ b/solution.py
@@ -24,6 +24,10 @@
     valid = wanted < rows_dev
     picked = table[jnp.minimum(wanted, rows_dev - 1)]
     return jnp.where(valid[..., None], picked, jnp.zeros_like(picked))
+
+
+def exchange(x):
+    return lax.all_to_all(x, AXES, split_axis=1, concat_axis=1, tiled=True)
 
 
 def local(
@@ -50,37 +54,42 @@
     cap_item = max(2, 2 * samples // devices)
     slots = cap + cap_item
     myself = lax.axis_index(AXES)
-    user_owner = hist_owner[:, 0]
-    goods_owner = item_owner[:, 0]
-    user_slot = slot_rank(user_owner, devices)
-    goods_slot = slot_rank(goods_owner, devices)
-    user_key = user_owner * slots + user_slot
-    goods_key = goods_owner * slots + cap + goods_slot
-    keys = jnp.concatenate([user_key, goods_key])
     entries = bag_weights.shape[0]
     segment = hist_seg[0]
-    row_bits = max(1, (rows_dev - 1).bit_length())
-    seg_bits = max(1, (samples - 1).bit_length())
-    packed = jnp.concatenate(
+    sample_ids = jnp.arange(samples, dtype=jnp.int32)
+    owner = jnp.concatenate([hist_owner[:, 0], item_owner[:, 0]])
+    rank = jnp.concatenate(
+        [slot_rank(hist_owner[:, 0], devices), cap + slot_rank(item_owner[:, 0], devices)]
+    )
+    row = jnp.concatenate([hist_row, item_row])
+    fields = jnp.stack(
         [
-            hist_row | (segment << row_bits) | (hist_wix << (row_bits + seg_bits)),
-            item_row | (jnp.arange(samples, dtype=jnp.int32) << row_bits),
+            row & 255,
+            row >> 8,
+            jnp.concatenate([segment, sample_ids]),
+            jnp.concatenate([hist_wix, jnp.zeros((samples,), jnp.int32)]),
+            jnp.ones_like(row),
         ]
     )
-    info = jnp.full((devices * slots,), -1, jnp.int32).at[keys].set(packed)
-    filled = info >= 0
-    req = jnp.where(filled, info & ((1 << row_bits) - 1), rows_dev).reshape(devices, slots)
-    slot_seg = (info >> row_bits) & ((1 << seg_bits) - 1)
-    slot_wix = info >> (row_bits + seg_bits)
-    is_user = (jnp.arange(devices * slots, dtype=jnp.int32) % slots) < cap
-    want = lax.all_to_all(req, AXES, split_axis=0, concat_axis=0, tiled=True)
-    user_want = want[:, :cap]
-    goods_want = want[:, cap:]
+    by_owner = (owner[None, :] == jnp.arange(devices, dtype=jnp.int32)[:, None]).astype(jnp.bfloat16)
+    planes = (fields.astype(jnp.bfloat16)[:, None, :] * by_owner[None, :, :]).reshape(-1, owner.shape[0])
+    by_rank = (rank[:, None] == jnp.arange(slots, dtype=jnp.int32)[None, :]).astype(jnp.bfloat16)
+    table = jnp.dot(planes, by_rank, preferred_element_type=jnp.float32)
+    table = table.astype(jnp.int32).reshape(fields.shape[0], devices, slots)
+    table = jnp.transpose(table, (0, 2, 1)).reshape(fields.shape[0], slots * devices)
+    slot_row = table[0] + 256 * table[1]
+    slot_seg = table[2]
+    slot_wix = table[3]
+    filled = table[4] > 0
+    req = jnp.where(filled, slot_row, rows_dev).reshape(slots, devices)
+    is_user = jnp.arange(slots * devices, dtype=jnp.int32) < cap * devices
+    want = exchange(req)
+    user_want = want[:cap]
+    goods_want = want[cap:]
     found = jnp.concatenate(
-        [lookup(user_table, user_want), lookup(item_table, goods_want)], axis=1
-    )
-    back = lax.all_to_all(found, AXES, split_axis=0, concat_axis=0, tiled=True)
-    back = back.reshape(devices * slots, width)
+        [lookup(user_table, user_want), lookup(item_table, goods_want)], axis=0
+    )
+    back = exchange(found).reshape(slots * devices, width)
     wts = jnp.sum(
         jnp.where(
             slot_wix[:, None] == jnp.arange(entries, dtype=jnp.int32)[None, :],
@@ -89,7 +98,6 @@
         ),
         1,
     ).astype(jnp.bfloat16)
-    sample_ids = jnp.arange(samples, dtype=jnp.int32)
     of_sample = filled[None, :] & (slot_seg[None, :] == sample_ids[:, None])
     member = of_sample & is_user[None, :]
     coef = jnp.where(member, wts[None, :], jnp.zeros((), jnp.bfloat16))
@@ -107,7 +115,7 @@
     uh_all = both[0]
     vh_all = both[1]
     total = vh_all.shape[0]
-    mine = myself * samples + jnp.arange(samples, dtype=jnp.int32)
+    mine = myself * samples + sample_ids
     everyone = jnp.arange(total, dtype=jnp.int32)
     scores = scale * jnp.dot(uh, vh_all.T, preferred_element_type=jnp.float32)
     top = jnp.max(scores, -1)
@@ -123,9 +131,9 @@
     d_bag = jnp.dot(d_u, user_proj.astype(jnp.float32).T, precision=highest)
     stats = jnp.concatenate([top, norm]).reshape(1, 1, -1)
     stats = jnp.broadcast_to(stats, (devices, 1, stats.shape[-1]))
-    user_parts = user_part.reshape(devices, -1, width)
     stats = jnp.pad(stats, ((0, 0), (0, 0), (0, -stats.shape[-1] % width)))
     stats = stats.reshape(devices, -1, width)
+    user_parts = user_part.reshape(devices, -1, width)
     n_stat = stats.shape[1]
     got_s = lax.all_to_all(
         jnp.concatenate([stats, user_parts], axis=1), AXES, split_axis=0, concat_axis=0, tiled=True
@@ -146,30 +154,31 @@
     g_slot = (wts.astype(jnp.float32) / per_slot[:, 2 * width])[:, None] * per_slot[:, :width]
     g_slot = jnp.where(is_user[:, None], g_slot, per_slot[:, width : 2 * width])
     g_slot = jnp.where(filled[:, None], g_slot, 0.0)
-    goods_parts = goods_part.reshape(devices, -1, width)
-    chunk = goods_parts.shape[1]
+    goods_parts = jnp.transpose(goods_part.reshape(devices, -1, width), (1, 0, 2))
+    chunk = goods_parts.shape[0]
     hi = goods_parts.astype(jnp.bfloat16)
     lo = (goods_parts - hi.astype(jnp.float32)).astype(jnp.bfloat16)
     send = jnp.concatenate(
-        [g_slot.astype(jnp.bfloat16).reshape(devices, slots, width), hi, lo], axis=1
-    )
-    got = lax.all_to_all(send, AXES, split_axis=0, concat_axis=0, tiled=True)
-    tail = got[:, slots:].astype(jnp.float32)
-    goods_red = jnp.sum(tail[:, :chunk] + tail[:, chunk:], 0)
+        [g_slot.astype(jnp.bfloat16).reshape(slots, devices, width), hi, lo], axis=0
+    )
+    got = exchange(send)
+    tail = got[slots:].astype(jnp.float32)
+    goods_red = jnp.sum(tail[:chunk] + tail[chunk:], 1)
     red = jnp.concatenate([user_red, goods_red])
-    padded = jnp.zeros((max(8, 2 * chunk), width), jnp.float32).at[: 2 * chunk].set(red)
-    gathered = lax.all_gather(padded, AXES, axis=0, tiled=True).reshape(devices, -1, width)
-    user_proj_grad = gathered[:, :chunk].reshape(width, width)
-    item_proj_grad = gathered[:, chunk : 2 * chunk].reshape(width, width)
+    spread = lax.all_to_all(
+        jnp.broadcast_to(red[None], (devices,) + red.shape), AXES, split_axis=0, concat_axis=0, tiled=True
+    )
+    user_proj_grad = spread[:, :chunk].reshape(width, width)
+    item_proj_grad = spread[:, chunk:].reshape(width, width)
     user_grad = (
         jnp.zeros((rows_dev, width), jnp.float32)
         .at[user_want.reshape(-1)]
-        .add(got[:, :cap].reshape(-1, width).astype(jnp.float32), mode="drop")
+        .add(got[:cap].reshape(-1, width).astype(jnp.float32), mode="drop")
     )
     item_grad = (
         jnp.zeros((rows_dev, width), jnp.float32)
         .at[goods_want.reshape(-1)]
-        .add(got[:, cap:slots].reshape(-1, width).astype(jnp.float32), mode="drop")
+        .add(got[cap:slots].reshape(-1, width).astype(jnp.float32), mode="drop")
     )
     return (user_grad, item_grad, user_proj_grad, item_proj_grad)
 

time: 366 us -> 324 us (0.89)
  waiting for transfers between devices: 191 us -> 159 us
  local copies, waits for them, and re-layouts: 46.7 us -> 34.1 us
  starting transfers between devices: 16.3 us -> 21.3 us
    all_gather x1 -> x0, waiting for transfers between devices: 31.6 us -> none  [local(): lax.all_gather(padded, AXES, axis=0, tiled=True).reshape(devices, -1, width)]
    scatter x1 -> x0, local copies, waits for them, and re-layouts: 11.2 us -> none  [local(): info = jnp.full((devices * slots,), -1, jnp.int32).at[keys].set(packed)]
    reshape x7 -> x5, local copies, waits for them, and re-layouts: 7.66 us -> 1.95 us  [the longest x1 0.88 us: local(): user_proj_grad = spread[:, :chunk].reshape(width, width)]
    all_to_all x2 -> x3, starting transfers between devices: 8.45 us -> 13.7 us  [the longest x2 8.32 us: exchange(): return lax.all_to_all(x, AXES, split_axis=1, concat_axis=1, tiled=True)]
    all_to_all x2 -> x3, waiting for transfers between devices: 67.8 us -> 68 us  [the longest x2 68 us: exchange(): return lax.all_to_all(x, AXES, split_axis=1, concat_axis=1, tiled=True)]
    gather x3 -> x2, local copies, waits for them, and re-layouts: 19.9 us -> 19.9 us  [lookup(): picked = table[jnp.minimum(wanted, rows_dev - 1)]]
  transfers between devices with their start and end apart: 5 -> 5, of which waited for: 5 -> 4; matrix products, arithmetic and copies ran while one was open for 9% -> 10% of each run, Pallas kernels for 0% -> 0%
where the time goes in v5:
time: 324 us; the launch traced here: 323 us
  waiting for transfers between devices  159 us (49%)
  other arithmetic  44 us (14%)
  local copies, waits for them, and re-layouts  34.1 us (11%)
  matrix products  28.3 us (9%)
  starting transfers between devices  21.3 us (7%)
  blocking collectives  21.1 us (7%)
  between operations  15.4 us (5%)
    all_gather x1, waiting for transfers between devices, local(): both = lax.all_gather(jnp.stack([uh, vh]), AXES, axis=1, tiled=True)  77.5 us
    all_to_all x2, waiting for transfers between devices, exchange(): return lax.all_to_all(x, AXES, split_axis=1, concat_axis=1, tiled=True)  68 us
    scatter-add x1, other arithmetic, local(): user_grad = jnp.zeros((rows_dev, width), jnp.float32).at[user_want.reshap...  23.3 us
    all_to_all x1, blocking collectives, exchange(): return lax.all_to_all(x, AXES, split_axis=1, concat_axis=1, tiled=True)  21.1 us
    gather x2, local copies, waits for them, and re-layouts, lookup(): picked = table[jnp.minimum(wanted, rows_dev - 1)]  19.9 us
    all_to_all x1, waiting for transfers between devices, local(): lax.all_to_all(jnp.concatenate([stats, user_parts], axis=1), AXES, split_...  13.6 us
    dot_general x1, matrix products, local(): jnp.dot(pw_c, uh_all, preferred_element_type=jnp.float32)  10.1 us
    all_to_all x2, starting transfers between devices, exchange(): return lax.all_to_all(x, AXES, split_axis=1, concat_axis=1, tiled=True)  8.32 us
  transfers between devices with their start and end apart: 5, of which 4 were waited for; matrix products, arithmetic and copies ran while one was open for 10% of the time, Pallas kernels for 0%

profile of v5, /device:TPU:1, one launch (start us, length us, event | category | flops | bytes accessed | tf_op | source)
XLA Modules:
  0.0 323.3 jit_solution(1996109544717540305)
XLA Ops:
  7.3 0.9 fusion.67
  8.3 0.8 select_reduce_fusion.1
  9.2 0.8 copy.71
  10.0 0.3 fusion.53
  10.4 0.3 copy.72
  10.8 0.6 fusion.52
  11.8 0.3 broadcast_multiply_fusion
  12.1 1.2 convolution_convert_fusion
  13.6 21.1 %all_to_all.26 = s32[34,128,1]{0,2,1:T(1,128)S(1)} all-to-all(s32[34,128,1]{0,2,1:T(1,128)S(1)} %copy.73), channel_id=1, replica_groups=mesh['dp'=8,'table'=16] {'dp','table'}, dimensions={1} | all-to-all | bytes 34816 | tf_op jit(solution)/shard_map/all_to_all | solution.py:30
  35.7 17.0 %gather_fusion = bf16[4096,256]{1,0:T(8,128)(2,1)} fusion(bf16[4096,256]{1,0:T(8,128)(2,1)S(1)} %copy-done, s32[4096]{0:T(1024)S(1)} %fusion.72), kind=kCustom, calls=%fused_computation | custom fusion | bytes 4210688 | tf_op jit(solution)/shard_map/gather | solution.py:25
  52.7 2.9 copy_select_fusion
  55.7 2.8 gather_fusion.1
  58.8 1.8 pad_maximum_fusion
  60.6 4.3 %all-to-all-start.1 = ((bf16[34,128,256]{2,0,1:T(8,128)(2,1)}), bf16[34,128,256]{2,0,1:T(8,128)(2,1)S(1)}, u32[]{:S(2)}, u32[]{:S(2)}) async-start(bf16[34,128,256]{2,0,1:T(8,128)(2,1)} %pad_maximum_fusion), calls=%async_computation.1 | async-start | bytes 5242880 | tf_op jit(solution)/shard_map/all_to_all | solution.py:30
  65.2 0.3 select_reduce_fusion
  65.5 0.6 convert_reduce_fusion
  66.1 33.5 %all-to-all-done.1 = bf16[34,128,256]{2,0,1:T(8,128)(2,1)S(1)} async-done(((bf16[34,128,256]{2,0,1:T(8,128)(2,1)}), bf16[34,128,256]{2,0,1:T(8,128)(2,1)S(1)}, u32[]{:S(2)}, u32[]{:S(2)}) %all-to-all-start.1) | async-done | bytes 2228256 | tf_op jit(solution)/shard_map/all_to_all | solution.py:30
  99.6 0.5 copy.81
  100.1 0.6 fusion.48
  100.7 0.3 multiply_reduce_fusion.3
  101.0 0.6 fusion.33
  102.0 0.7 pad_maximum_fusion.3
  103.3 77.5 %all-gather.2.cloned.1.call-done = bf16[2,16384,256]{2,1,0:T(8,128)(2,1)} async-done(((bf16[2,128,256]{2,1,0:T(8,128)(2,1)}), bf16[2,16384,256]{2,1,0:T(8,128)(2,1)}) %all-gather.2.cloned.1.call-update) | async-done | bytes 16777232 | tf_op jit(solution)/shard_map/all_gather | solution.py:114
  180.8 5.3 %fusion.82 = (f32[128]{0:T(128)S(1)}, f32[128,16384]{1,0:T(8,128)S(1)}) fusion(bf16[2,16384,256]{2,1,0:T(8,128)(2,1)} %all-gather.2.cloned.1.call-done, f32[128,256]{1,0:T(8,128)S(1)} %get-tuple-element.18, f32[128]{0:T(128)S(1)} %add_rsqrt_fusion.1, f32[]{:T(128)} %bitcast.102), kind=kOutput, calls=%fused_computation.148 | convolution fusion | flops 1078001536 | bytes 16909824 | tf_op jit(solution)/shard_map/dot_general | solution.py:120
  186.2 1.6 fusion.6
  187.7 5.2 %multiply_reduce_fusion.1 = (f32[128]{0:T(128)S(1)}, f32[128,256]{1,0:T(8,128)S(1)}) fusion(f32[128,256]{1,0:T(8,128)S(1)} %get-tuple-element.18, f32[128]{0:T(128)S(1)} %add_rsqrt_fusion.1, bf16[2,16384,256]{2,1,0:T(8,128)(2,1)} %all-gather.2.cloned.1.call-done, f32[128,16384]{1,0:T(8,128)S(1)} %get-tuple-element.20, s32[128]{0:T(128)S(1)} %iota_add_fusion, ...), kind=kOutput, calls=%fused_computation.96 | convolution fusion | flops 1086455680 | bytes 17041924 | tf_op jit(solution)/shard_map/dot_general | solution.py:127
  192.9 0.4 fusion.78
  193.5 1.0 pad_maximum_fusion.2
  194.6 7.4 %all-to-all-start.2 = ((f32[128,3,256]{2,1,0:T(4,128)}), f32[128,3,256]{2,1,0:T(4,128)S(1)}, u32[]{:S(2)}, u32[]{:S(2)}) async-start(f32[128,3,256]{2,1,0:T(4,128)} %pad_maximum_fusion.2), calls=%async_computation.2 | async-start | bytes 1048576 | tf_op jit(solution)/shard_map/all_to_all | solution.py:138
  202.1 0.3 fusion.79
  202.4 13.6 %all-to-all-done.2 = f32[128,3,256]{2,1,0:T(4,128)S(1)} async-done(((f32[128,3,256]{2,1,0:T(4,128)}), f32[128,3,256]{2,1,0:T(4,128)S(1)}, u32[]{:S(2)}, u32[]{:S(2)}) %all-to-all-start.2) | async-done | bytes 393248 | tf_op jit(solution)/shard_map/all_to_all | solution.py:138
  216.1 10.1 %multiply_reduce_fusion = (f32[128]{0:T(128)S(1)}, f32[128,256]{1,0:T(8,128)S(1)}) fusion(f32[128,256]{1,0:T(8,128)S(1)} %get-tuple-element.16, f32[128]{0:T(128)S(1)} %add_rsqrt_fusion, bf16[2,16384,256]{2,1,0:T(8,128)(2,1)} %all-gather.2.cloned.1.call-done, f32[16384]{0:T(1024)S(1)} %get-tuple-element.10, f32[16384]{0:T(1024)S(1)} %get-tuple-element.9, ...), kind=kOutput, calls=%fused_computation.94 | convolution fusion | flops 2162360320 | bytes 17303560 | tf_op jit(solution)/shard_map/dot_general | solution.py:149
  226.3 0.3 fusion.83
  226.8 3.8 %fusion.17 = f32[4352,513]{0,1:T(8,128)S(1)} fusion(s32[4352]{0:T(1024)S(1)} %bitcast.120, pred[4352]{0:T(1024)(128)(4,1)S(1)} %bitcast.125, f32[128,1]{1,0:T(8,128)S(1)} %copy.82, f32[128,256]{1,0:T(8,128)S(1)} %subtract_multiply_fusion, f32[128,256]{1,0:T(8,128)S(1)} %fusion.79), kind=kOutput, calls=%fused_computation.33 | convolution fusion | flops 3430482176 | bytes 9214720 | tf_op jit(solution)/shard_map/dot_general | solution.py:153
  230.7 0.6 fusion.10
  231.3 2.4 copy.83
  233.7 1.9 pad_maximum_fusion.1
  235.6 2.9 copy.85
  238.6 4.0 %all-to-all-start.3 = ((bf16[38,128,256]{2,0,1:T(8,128)(2,1)}), bf16[38,128,256]{2,0,1:T(8,128)(2,1)S(1)}, u32[]{:S(2)}, u32[]{:S(2)}) async-start(bf16[38,128,256]{2,0,1:T(8,128)(2,1)} %copy.85), calls=%async_computation.3 | async-start | bytes 5242880 | tf_op jit(solution)/shard_map/all_to_all | solution.py:30
  242.8 34.6 %all-to-all-done.3 = bf16[38,128,256]{2,0,1:T(8,128)(2,1)S(1)} async-done(((bf16[38,128,256]{2,0,1:T(8,128)(2,1)}), bf16[38,128,256]{2,0,1:T(8,128)(2,1)S(1)}, u32[]{:S(2)}, u32[]{:S(2)}) %all-to-all-start.3) | async-done | bytes 2490400 | tf_op jit(solution)/shard_map/all_to_all | solution.py:30
  277.7 0.9 broadcast_in_dim.137
  278.6 5.4 %all-to-all-start.4 = ((f32[128,4,256]{2,1,0:T(4,128)}), f32[128,4,256]{2,1,0:T(4,128)S(1)}, u32[]{:S(2)}, u32[]{:S(2)}) async-start(f32[128,4,256]{2,1,0:T(4,128)} %broadcast_in_dim.137), calls=%async_computation.4 | async-start | bytes 1048576 | tf_op jit(solution)/shard_map/all_to_all | solution.py:168
  284.2 0.3 slice.128
  284.5 2.6 copy.91
  287.0 4.2 %scatter_custom_fusion.1 = f32[4096,256]{1,0:T(8,128)} fusion(s32[256]{0:T(256)S(1)} %bitcast.140, f32[]{:T(128)} %constant.18.clone.1, bf16[256,256]{1,0:T(8,128)(2,1)S(1)} %bitcast.112), kind=kCustom, calls=%fused_computation.39 | custom fusion | flops 131072 | bytes 4325380 | tf_op jit(solution)/shard_map/scatter-add | solution.py:181
  291.2 23.3 %scatter_custom_fusion = f32[4096,256]{1,0:T(8,128)} fusion(s32[4096]{0:T(1024)S(1)} %bitcast.131, bf16[4096,256]{1,0:T(8,128)(2,1)} %bitcast.106, f32[]{:T(128)} %constant.18.clone.1), kind=kCustom, calls=%fused_computation.24 | custom fusion | flops 2097152 | bytes 6291460 | tf_op jit(solution)/shard_map/scatter-add | solution.py:176
  314.7 0.9 reshape.397
  315.6 0.9 reshape.398
  (90 shorter events, 4.6 us)
Async XLA Ops:
  7.2 28.5 %copy-start = (bf16[4096,256]{1,0:T(8,128)(2,1)S(1)}, bf16[4096,256]{1,0:T(8,128)(2,1)}, u32[]{:S(2)}) copy-start(bf16[4096,256]{1,0:T(8,128)(2,1)} %param.12) | copy-start | bytes 6291460
  7.2 3.6 %copy-start.8 = (s32[128,1]{0,1:T(1,128)S(1)}, s32[128,1]{0,1:T(1,128)}, u32[]{:S(2)}) copy-start(s32[128,1]{0,1:T(1,128)} %param.19) | copy-start | bytes 1540
  7.2 3.6 %copy-start.4 = (s32[2048,1]{0,1:T(1,128)S(1)}, s32[2048,1]{0,1:T(1,128)}, u32[]{:S(2)}) copy-start(s32[2048,1]{0,1:T(1,128)} %param.14) | copy-start | bytes 24580
  7.2 4.3 %copy-start.6 = (s32[1,2048]{1,0:T(1,128)S(1)}, s32[1,2048]{1,0:T(1,128)}, u32[]{:S(2)}) copy-start(s32[1,2048]{1,0:T(1,128)} %param.16) | copy-start | bytes 24580
  7.2 4.4 %copy-start.7 = (s32[2048]{0:T(1024)S(1)}, s32[2048]{0:T(1024)}, u32[]{:S(2)}) copy-start(s32[2048]{0:T(1024)} %param.17) | copy-start | bytes 24580
  7.2 4.5 %copy-start.5 = (s32[2048]{0:T(1024)S(1)}, s32[2048]{0:T(1024)}, u32[]{:S(2)}) copy-start(s32[2048]{0:T(1024)} %param.15) | copy-start | bytes 24580
  7.2 4.5 %copy-start.9 = (s32[128]{0:T(128)S(1)}, s32[128]{0:T(128)}, u32[]{:S(2)}) copy-start(s32[128]{0:T(128)} %param.20) | copy-start | bytes 1540
  58.8 6.3 %copy-start.10 = (bf16[64]{0:T(256)(128)(2,1)S(1)}, bf16[64]{0:T(256)(128)(2,1)}, u32[]{:S(2)}) copy-start(bf16[64]{0:T(256)(128)(2,1)} %param.18) | copy-start | bytes 388
  60.6 39.0 %all-to-all-start.1 = ((bf16[34,128,256]{2,0,1:T(8,128)(2,1)}), bf16[34,128,256]{2,0,1:T(8,128)(2,1)S(1)}, u32[]{:S(2)}, u32[]{:S(2)}) async-start(bf16[34,128,256]{2,0,1:T(8,128)(2,1)} %pad_maximum_fusion), calls=%async_computation.1 | async-start | bytes 5242880 | tf_op jit(solution)/shard_map/all_to_all | solution.py:30
  64.9 116.0 %all-gather.2.cloned.1.call-start = ((), (), s32[]{:S(2)}) async-start(), calls=%async_computation.5 | async-start | bytes 16908288 | tf_op jit(solution)/shard_map/all_gather | solution.py:114
  66.1 34.6 %copy-start.2 = (bf16[256,256]{1,0:T(8,128)(2,1)S(1)}, bf16[256,256]{1,0:T(8,128)(2,1)}, u32[]{:S(2)}) copy-start(bf16[256,256]{1,0:T(8,128)(2,1)} %param.21) | copy-start | bytes 393220
  100.1 1.5 copy-start.3
  194.6 21.4 %all-to-all-start.2 = ((f32[128,3,256]{2,1,0:T(4,128)}), f32[128,3,256]{2,1,0:T(4,128)S(1)}, u32[]{:S(2)}, u32[]{:S(2)}) async-start(f32[128,3,256]{2,1,0:T(4,128)} %pad_maximum_fusion.2), calls=%async_computation.2 | async-start | bytes 1048576 | tf_op jit(solution)/shard_map/all_to_all | solution.py:138
  238.6 38.8 %all-to-all-start.3 = ((bf16[38,128,256]{2,0,1:T(8,128)(2,1)}), bf16[38,128,256]{2,0,1:T(8,128)(2,1)S(1)}, u32[]{:S(2)}, u32[]{:S(2)}) async-start(bf16[38,128,256]{2,0,1:T(8,128)(2,1)} %copy.85), calls=%async_computation.3 | async-start | bytes 5242880 | tf_op jit(solution)/shard_map/all_to_all | solution.py:30
  278.6 35.9 %all-to-all-start.4 = ((f32[128,4,256]{2,1,0:T(4,128)}), f32[128,4,256]{2,1,0:T(4,128)S(1)}, u32[]{:S(2)}, u32[]{:S(2)}) async-start(f32[128,4,256]{2,1,0:T(4,128)} %broadcast_in_dim.137), calls=%async_computation.4 | async-start | bytes 1048576 | tf_op jit(solution)/shard_map/all_to_all | solution.py:168
  291.2 25.2 %copy-start.1 = (bf16[4096,256]{1,0:T(8,128)(2,1)S(1)}, bf16[4096,256]{1,0:T(8,128)(2,1)}, u32[]{:S(2)}) copy-start(bf16[4096,256]{1,0:T(8,128)(2,1)} %param.12) | copy-start | bytes 6291460
Sparse Core Ops, SparseCore 0:
  102.8 78.0 all-gather.1
